TPU v7x, 32 devices: a whole 2x2x4 slice. The times are simulated.
32 devices in a mesh: region: 2 (over y), mod: 4 (over z), obs: 4 (over x, core).
Axes of the slice: x: 2, y: 2, z: 4, core: 2. Of those that a mesh axis runs over, the one named last changes fastest.
Arguments:
- model_days: float32 [16384, 128], P(('region', 'mod')), parts along dimension 0, may hold values from -48 to 48
- obs_days: float32 [16384, 128], P(('region', 'obs', 'mod')), parts along dimension 0, may hold values from -48 to 48
Outputs:
- mapped: float32 [16384, 128], P(('region', 'mod', 'obs')), parts along dimension 0
- row_potential: float32 [16384], P(('region', 'mod')), parts along dimension 0
- col_potential: float32 [16384], P(('region', 'obs')), parts along dimension 0
There are 2 independent parts, one for each index of `region`. A program takes and returns all parts, laid end to end along the dimension named above; each array names one. Nothing has to cross between parts.
All inputs are finite; a program needn't handle non-finite values.
Results may differ from a plain program's by a relative error of at most 0.0003.
Values sent between devices are 32-bit elements; how exact they have to be, the bound alone decides.
No kernel may reach another device: no remote copies, remote signals or barrier semaphores. Data moves between devices by JAX's collectives and lax.ppermute only.
A program may use at most 64 MiB of HBM per device.

v0:
```python
import math

import jax
import jax.numpy as jnp
from jax import lax
from jax.experimental import pallas as pl
from jax.experimental.pallas import tpu as pltpu
from jax.sharding import PartitionSpec as P

ITERS = 2

INV_E = 50.0
RB = 8


def _lane_tiles(s):
    return [s[:, j * 128:(j + 1) * 128] for j in range(s.shape[1] // 128)]

def _row_pass_max(h, c_ref, m_scr, tr):
    def p1(i, carry):
        r = pl.multiple_of(i * RB, RB)
        tiles = _lane_tiles((h - c_ref[pl.ds(r, RB), :]) * INV_E)
        m = tiles[0]
        for t in tiles[1:]:
            m = jnp.maximum(m, t)
        m_scr[pl.ds(r, RB), :] = m
        return carry
    lax.fori_loop(0, tr // RB, p1, 0, unroll=4)
    return jnp.max(m_scr[...], axis=1, keepdims=True)

FB = 8
def _final_kernel(h_ref, c_ref, y_ref, m_ref, l_ref, p_ref, w_ref, m_scr, t_scr):
    h = h_ref[...]
    tr = c_ref.shape[0]
    m_ref[...] = _row_pass_max(h, c_ref, m_scr, tr)
    def p2(i, carry):
        r = pl.multiple_of(i * RB, RB)
        mr = m_ref[pl.ds(r, RB), :]
        w = jnp.exp((h - c_ref[pl.ds(r, RB), :]) * INV_E - mr)
        w_ref[pl.ds(r, RB), :] = w
        tiles = _lane_tiles(w)
        t = tiles[0]
        for u in tiles[1:]:
            t = t + u
        t_scr[pl.ds(r, RB), :] = t
        return carry
    lax.fori_loop(0, tr // RB, p2, 0, unroll=4)
    l_ref[...] = m_ref[...] + jnp.log(jnp.sum(t_scr[...], axis=1, keepdims=True))
    w = w_ref[...]
    wh = w.astype(jnp.bfloat16)
    wl = (w - wh.astype(jnp.float32)).astype(jnp.bfloat16)
    y = y_ref[...]
    yh = y.astype(jnp.bfloat16)
    yl = (y - yh.astype(jnp.float32)).astype(jnp.bfloat16)
    acc = jnp.dot(wh, yh, preferred_element_type=jnp.float32)
    acc = acc + jnp.dot(wh, yl, preferred_element_type=jnp.float32)
    acc = acc + jnp.dot(wl, yh, preferred_element_type=jnp.float32)
    p_ref[...] = acc

def final_local(h, cost, y, tr=256):
    R, C = cost.shape
    F = y.shape[1]
    m, l, p = pl.pallas_call(
        _final_kernel,
        grid=(R // tr,),
        in_specs=[pl.BlockSpec((1, C), lambda i: (0, 0)), pl.BlockSpec((tr, C), lambda i: (i, 0)),
                  pl.BlockSpec((C, F), lambda i: (0, 0))],
        out_specs=[pl.BlockSpec((tr, 1), lambda i: (i, 0)), pl.BlockSpec((tr, 1), lambda i: (i, 0)),
                   pl.BlockSpec((tr, F), lambda i: (i, 0))],
        out_shape=[jax.ShapeDtypeStruct((R, 1), jnp.float32), jax.ShapeDtypeStruct((R, 1), jnp.float32),
                   jax.ShapeDtypeStruct((R, F), jnp.float32)],
        scratch_shapes=[pltpu.VMEM((tr, C), jnp.float32), pltpu.VMEM((tr, 128), jnp.float32), pltpu.VMEM((tr, 128), jnp.float32)],
    )(h.reshape(1, C), cost, y)
    return m.reshape(R), l.reshape(R), p


entropy_scale = 0.02


def shift_pairs(n, s):
    return [(i, (i + s) % n) for i in range(n)]


def pair_cost(block_rows, block_square, columns):
    column_square = jnp.sum(columns * columns, axis=1)
    cross = lax.dot_general(
        block_rows,
        columns,
        (((1,), (1,)), ((), ())),
        precision=lax.Precision.HIGHEST,
        preferred_element_type=jnp.float32,
    )
    return (block_square[:, None] + column_square[None, :] - 2.0 * cross) / block_rows.shape[1]


def lse_across(local_lse, axis):
    n = lax.axis_size(axis)
    vals = [local_lse] + [lax.ppermute(local_lse, axis, shift_pairs(n, s)) for s in range(1, n)]
    stacked = jnp.stack(vals)
    top = jnp.max(stacked, axis=0)
    return top + jnp.log(jnp.sum(jnp.exp(stacked - top[None]), axis=0))


def reorder(vec, order):
    n = order.shape[0]
    return jnp.take(vec.reshape(n, -1), order, axis=0).reshape(-1)


def scatter_obs(partial):
    n = lax.axis_size("obs")
    half = n // 2
    o = lax.axis_index("obs")
    x = o // 2
    c = o % 2
    share = partial.shape[0] // n
    p4 = partial.reshape(half, 2, share, partial.shape[1])
    keep = lax.dynamic_index_in_dim(p4, c, axis=1, keepdims=False)
    give = lax.dynamic_index_in_dim(p4, 1 - c, axis=1, keepdims=False)
    acc = keep + lax.ppermute(give, "obs", [(i, i ^ 1) for i in range(n)])
    total = lax.dynamic_index_in_dim(acc, x, axis=0, keepdims=False)
    for k in range(1, half):
        pairs = [(i, ((i // 2 + k) % half) * 2 + i % 2) for i in range(n)]
        piece = lax.dynamic_index_in_dim(acc, (x + k) % half, axis=0, keepdims=False)
        total = total + lax.ppermute(piece, "obs", pairs)
    return total


def on_device(model_days, obs_days):
    row_square = jnp.sum(model_days * model_days, axis=1)
    row_count = model_days.shape[0]
    n_mod = lax.axis_size("mod")
    m = lax.axis_index("mod")
    col_count = obs_days.shape[0] * n_mod
    log_obs = math.log(col_count * lax.axis_size("obs"))
    log_model = math.log(row_count * n_mod)
    blocks = [obs_days] + [
        lax.ppermute(obs_days, "mod", shift_pairs(n_mod, s)) for s in range(1, n_mod)
    ]
    order = (m - jnp.arange(n_mod)) % n_mod
    gathered = jnp.concatenate(blocks, axis=0)
    cost_tile = jnp.concatenate(
        [pair_cost(model_days, row_square, b) for b in blocks], axis=1
    )

    def row_lse(col_potential):
        scores = (col_potential[None, :] - cost_tile) / entropy_scale
        peaks = jnp.max(scores, axis=1)
        local = peaks + jnp.log(jnp.sum(jnp.exp(scores - peaks[:, None]), axis=1))
        return lse_across(local, "obs")

    col_shift = jnp.zeros((col_count,), jnp.float32)
    for iteration in range(ITERS):
        row_potential = -entropy_scale * (row_lse(col_shift) - log_obs)
        col_scores = (row_potential[:, None] - cost_tile) / entropy_scale
        col_peaks = jnp.max(col_scores, axis=0)
        local = col_peaks + jnp.log(jnp.sum(jnp.exp(col_scores - col_peaks[None, :]), axis=0))
        col_global = lse_across(reorder(local, order), "mod")
        col_potential = -entropy_scale * (col_global - log_model)
        col_shift = reorder(col_potential, order)
    peaks, local, partial_map = final_local(col_shift, cost_tile, gathered)
    final_lse = lse_across(local, "obs")
    row_potential = -entropy_scale * (final_lse - log_obs)
    mapped = scatter_obs(partial_map * jnp.exp(peaks - final_lse)[:, None])
    return (mapped, row_potential, col_potential)


def solution(mesh):
    in_specs = (P(("region", "mod"), None), P(("region", "obs", "mod"), None))
    out_specs = (P(("region", "mod", "obs"), None), P(("region", "mod")), P(("region", "obs")))
    return jax.shard_map(
        on_device, mesh=mesh, in_specs=in_specs, out_specs=out_specs, check_vma=False
    )
```

profile of v0, /device:TPU:0, one launch (start us, length us, event | category | flops | bytes accessed | tf_op | source)
XLA Modules:
  0.0 152.5 jit_solution(4574170251231086967)
XLA Ops:
  0.6 4.1 %collective-permute-start.1 = (f32[512,128]{1,0:T(8,128)}, f32[512,128]{1,0:T(8,128)S(1)}, u32[]{:S(2)}, u32[]{:S(2)}) collective-permute-start(f32[512,128]{1,0:T(8,128)} %param.5), channel_id=1, source_target_pairs={{0,8},{4,12},{8,0},{12,4},{1,9},{5,13},{9,1},{13,5},{2,10},{6,14},... | collective-permute-start | bytes 786440 | tf_op jit(solution)/shard_map/ppermute | solution.py:137
  4.8 1.6 %collective-permute-start = (f32[512,128]{1,0:T(8,128)}, f32[512,128]{1,0:T(8,128)S(1)}, u32[]{:S(2)}, u32[]{:S(2)}) collective-permute-start(f32[512,128]{1,0:T(8,128)} %param.5), channel_id=1, source_target_pairs={{0,4},{4,8},{8,12},{12,0},{1,5},{5,9},{9,13},{13,1},{2,6},{6,10},{... | collective-permute-start | bytes 786440 | tf_op jit(solution)/shard_map/ppermute | solution.py:137
  6.3 2.2 %collective-permute-start.2 = (f32[512,128]{1,0:T(8,128)}, f32[512,128]{1,0:T(8,128)S(1)}, u32[]{:S(2)}, u32[]{:S(2)}) collective-permute-start(f32[512,128]{1,0:T(8,128)} %param.5), channel_id=1, source_target_pairs={{0,12},{4,0},{8,4},{12,8},{1,13},{5,1},{9,5},{13,9},{2,14},{6,2},{... | collective-permute-start | bytes 786440 | tf_op jit(solution)/shard_map/ppermute | solution.py:137
  11.3 5.0 %subtract_multiply_fusion.7 = f32[2048,512]{1,0:T(8,128)S(1)} fusion(f32[2048,128]{1,0:T(8,128)} %param.4, f32[512,128]{1,0:T(8,128)} %param.5, f32[512]{0:T(512)S(1)} %multiply_reduce_fusion.4, f32[2048]{0:T(1024)S(1)} %multiply_reduce_fusion), kind=kOutput, calls=%fused_computation.20 | convolution fusion | flops 1614807040 | bytes 5515264 | tf_op jit(solution)/shard_map/dot_general | solution.py:86
  16.4 7.0 %collective-permute-done.1 = f32[512,128]{1,0:T(8,128)S(1)} collective-permute-done((f32[512,128]{1,0:T(8,128)}, f32[512,128]{1,0:T(8,128)S(1)}, u32[]{:S(2)}, u32[]{:S(2)}) %collective-permute-start.1) | collective-permute-done | bytes 262176 | tf_op jit(solution)/shard_map/ppermute | solution.py:137
  23.6 5.0 %subtract_multiply_fusion.5 = f32[2048,512]{1,0:T(8,128)S(1)} fusion(f32[2048,128]{1,0:T(8,128)} %param.4, f32[512,128]{1,0:T(8,128)S(1)} %collective-permute-done.1, f32[512]{0:T(512)S(1)} %multiply_reduce_fusion.2, f32[2048]{0:T(1024)S(1)} %multiply_reduce_fusion), kind=kOutput, calls=%fused_computation.18 | convolution fusion | flops 1614807040 | bytes 5515264 | tf_op jit(solution)/shard_map/dot_general | solution.py:86
  28.7 5.9 %subtract_multiply_fusion.6 = f32[2048,512]{1,0:T(8,128)S(1)} fusion(f32[2048,128]{1,0:T(8,128)} %param.4, f32[512,128]{1,0:T(8,128)S(1)} %collective-permute-done, f32[512]{0:T(512)S(1)} %multiply_reduce_fusion.3, f32[2048]{0:T(1024)S(1)} %multiply_reduce_fusion), kind=kOutput, calls=%fused_computation.19 | convolution fusion | flops 1614807040 | bytes 5515264 | tf_op jit(solution)/shard_map/dot_general | solution.py:86
  34.8 3.7 %subtract_multiply_fusion.4 = f32[2048,512]{1,0:T(8,128)S(1)} fusion(f32[2048,128]{1,0:T(8,128)S(1)} %copy-done.8, f32[512,128]{1,0:T(8,128)S(1)} %collective-permute-done.2, f32[512]{0:T(512)S(1)} %multiply_reduce_fusion.1, f32[2048]{0:T(1024)S(1)} %multiply_reduce_fusion), kind=kOutput, calls=%fused_computation.17 | convolution fusion | flops 1614807040 | bytes 5515264 | tf_op jit(solution)/shard_map/dot_general | solution.py:86
  38.6 7.0 %pad_maximum_fusion = (f32[2048,2048]{1,0:T(8,128)}, f32[2048]{0:T(1024)S(1)}) fusion(f32[2048,512]{1,0:T(8,128)S(1)} %subtract_multiply_fusion.4, f32[2048,512]{1,0:T(8,128)S(1)} %subtract_multiply_fusion.5, f32[2048,512]{1,0:T(8,128)S(1)} %subtract_multiply_fusion.6, f32[2048,512]{1,0:T(8,128)S(1)} %subtract_multiply_fusion.7), kind=kLoop, calls=%fused_computation.4 | loop fusion | flops 25163776 | bytes 33562624 | tf_op jit(solution)/shard_map/concatenate | solution.py:141
  45.6 4.4 %exponential_reduce_fusion.3 = f32[2048]{0:T(1024)S(1)} fusion(f32[2048]{0:T(1024)S(1)} %get-tuple-element.11, f32[2048,512]{1,0:T(8,128)S(1)} %subtract_multiply_fusion.4, f32[2048,512]{1,0:T(8,128)S(1)} %subtract_multiply_fusion.5, f32[2048,512]{1,0:T(8,128)S(1)} %subtract_multiply_fusion.6, f32[2048,512]{1,0:T(8,128)S(1)} %subtract_multiply_fusion.7), kind=kLoop, calls=%fused_computation.11 | loop fusion | flops 29358080 | bytes 16793600 | tf_op jit(solution)/shard_map/reduce_sum | solution.py:148
  50.0 1.9 %collective-permute-start.4 = (f32[2048]{0:T(1024)S(1)}, f32[2048]{0:T(1024)S(1)}, u32[]{:S(2)}, u32[]{:S(2)}) collective-permute-start(f32[2048]{0:T(1024)S(1)} %log_add_fusion.3), channel_id=1, source_target_pairs={{0,2},{1,3},{2,0},{3,1},{4,6},{5,7},{6,4},{7,5},{8,10},{9,11},{10,... | collective-permute-start | bytes 24584 | tf_op jit(solution)/shard_map/ppermute | solution.py:98
  54.7 2.5 %fusion.1 = f32[2048]{0:T(1024)S(1)} fusion(f32[2048]{0:T(1024)S(1)} %add_multiply_fusion.5, f32[2048,512]{1,0:T(8,128)S(1)} %subtract_multiply_fusion.4, f32[2048,512]{1,0:T(8,128)S(1)} %subtract_multiply_fusion.5, f32[2048,512]{1,0:T(8,128)S(1)} %subtract_multiply_fusion.6, f32[2048,512]{1,0:T(8,128)S(1)} %subtract_multiply_fusion.7), kind=kLoop, calls=%fused_computation.14 | loop fusion | flops 25163776 | bytes 16793600 | tf_op jit(solution)/shard_map/reduce_max | solution.py:155
  57.3 4.5 %exponential_reduce_fusion.2 = f32[2048]{0:T(1024)S(1)} fusion(f32[2048]{0:T(1024)S(1)} %fusion.1, f32[2048]{0:T(1024)S(1)} %add_multiply_fusion.5, f32[2048,512]{1,0:T(8,128)S(1)} %subtract_multiply_fusion.4, f32[2048,512]{1,0:T(8,128)S(1)} %subtract_multiply_fusion.5, f32[2048,512]{1,0:T(8,128)S(1)} %subtract_multiply_fusion.6, ...), kind=kLoop, calls=%fused_computation.9 | loop fusion | flops 29358080 | bytes 16801792 | tf_op jit(solution)/shard_map/reduce_sum | solution.py:156
  63.6 2.9 %collective-permute-start.8 = (f32[2048]{0:T(1024)S(1)}, f32[2048]{0:T(1024)S(1)}, u32[]{:S(2)}, u32[]{:S(2)}) collective-permute-start(f32[2048]{0:T(1024)S(1)} %bitcast.87), channel_id=1, source_target_pairs={{0,12},{4,0},{8,4},{12,8},{1,13},{5,1},{9,5},{13,9},{2,14},{6,2},{... | collective-permute-start | bytes 24584 | tf_op jit(solution)/shard_map/ppermute | solution.py:98
  69.3 8.0 %fusion.2 = f32[2048]{0:T(1024)S(1)} fusion(f32[2048]{0:T(1024)S(1)} %bitcast.62, f32[2048,512]{1,0:T(8,128)} %copy-done.6, f32[2048,512]{1,0:T(8,128)} %copy-done.2, f32[2048,512]{1,0:T(8,128)} %copy-done.4, f32[2048,512]{1,0:T(8,128)} %copy-done), kind=kLoop, calls=%fused_computation.15 | loop fusion | flops 25163776 | bytes 16793600 | tf_op jit(solution)/shard_map/reduce_max | solution.py:147
  80.0 4.4 %exponential_reduce_fusion.1 = f32[2048]{0:T(1024)S(1)} fusion(f32[2048]{0:T(1024)S(1)} %fusion.2, f32[2048]{0:T(1024)S(1)} %bitcast.63, f32[2048,512]{1,0:T(8,128)S(1)} %copy-done.7, f32[2048,512]{1,0:T(8,128)S(1)} %copy-done.3, f32[2048,512]{1,0:T(8,128)S(1)} %copy-done.5, f32[2048,512]{1,0:T(8,128)S(1)} %copy-done.1), kind=kLoop, calls=%fused_computation.7 | loop fusion | flops 29358080 | bytes 16801792 | tf_op jit(solution)/shard_map/reduce_sum | solution.py:148
  86.0 2.2 %collective-permute-done.10 = f32[2048]{0:T(1024)S(1)} collective-permute-done((f32[2048]{0:T(1024)S(1)}, f32[2048]{0:T(1024)S(1)}, u32[]{:S(2)}, u32[]{:S(2)}) %collective-permute-start.10) | collective-permute-done | bytes 8224 | tf_op jit(solution)/shard_map/ppermute | solution.py:98
  88.7 2.5 %fusion.3 = f32[2048]{0:T(1024)S(1)} fusion(f32[2048]{0:T(1024)S(1)} %add_multiply_fusion.3, f32[2048,512]{1,0:T(8,128)S(1)} %copy-done.7, f32[2048,512]{1,0:T(8,128)S(1)} %copy-done.3, f32[2048,512]{1,0:T(8,128)S(1)} %copy-done.5, f32[2048,512]{1,0:T(8,128)S(1)} %copy-done.1), kind=kLoop, calls=%fused_computation.16 | loop fusion | flops 25163776 | bytes 16793600 | tf_op jit(solution)/shard_map/reduce_max | solution.py:155
  91.2 4.6 %exponential_reduce_fusion = f32[2048]{0:T(1024)S(1)} fusion(f32[2048]{0:T(1024)S(1)} %fusion.3, f32[2048]{0:T(1024)S(1)} %add_multiply_fusion.3, f32[2048,512]{1,0:T(8,128)S(1)} %copy-done.7, f32[2048,512]{1,0:T(8,128)S(1)} %copy-done.3, f32[2048,512]{1,0:T(8,128)S(1)} %copy-done.5, f32[2048,512]{1,0:T(8,128)S(1)} %copy-done.1), kind=kLoop, calls=%fused_computation.5 | loop fusion | flops 29358080 | bytes 16801792 | tf_op jit(solution)/shard_map/reduce_sum | solution.py:156
  96.5 1.9 %collective-permute-start.12 = (f32[2048]{0:T(1024)S(1)}, f32[2048]{0:T(1024)S(1)}, u32[]{:S(2)}, u32[]{:S(2)}) collective-permute-start(f32[2048]{0:T(1024)S(1)} %bitcast.81), channel_id=1, source_target_pairs={{0,4},{4,8},{8,12},{12,0},{1,5},{5,9},{9,13},{13,1},{2,6},{6,10},{... | collective-permute-start | bytes 24584 | tf_op jit(solution)/shard_map/ppermute | solution.py:98
  98.4 2.0 %collective-permute-start.13 = (f32[2048]{0:T(1024)S(1)}, f32[2048]{0:T(1024)S(1)}, u32[]{:S(2)}, u32[]{:S(2)}) collective-permute-start(f32[2048]{0:T(1024)S(1)} %bitcast.82), channel_id=1, source_target_pairs={{0,8},{4,12},{8,0},{12,4},{1,9},{5,13},{9,1},{13,5},{2,10},{6,14},... | collective-permute-start | bytes 24584 | tf_op jit(solution)/shard_map/ppermute | solution.py:98
  106.1 21.7 %shard_map.49 = (f32[2048,1]{1,0:T(8,128)}, f32[2048,1]{1,0:T(8,128)}, f32[2048,128]{1,0:T(8,128)}) custom-call(f32[1,2048]{1,0:T(1,128)} %bitcast.79, f32[2048,2048]{1,0:T(8,128)} %get-tuple-element.10.c_ref, f32[2048,128]{1,0:T(8,128)} %pad_maximum_fusion.1.y_ref), custom_call_target="tpu_custom_call" | custom-call | tf_op jit(solution)/shard_map/pallas_call | solution.py:63
  136.6 2.2 %exponential_reduce_fusion.4 = f32[2048]{0:T(1024)S(1)} fusion(f32[2048,1]{1,0:T(8,128)} %get-tuple-element.8, f32[2048,1]{1,0:T(8,128)S(1)} %copy.24, f32[2048,1]{1,0:T(8,128)} %copy.23, f32[2048,1]{1,0:T(8,128)S(1)} %copy.22, f32[2048,1]{1,0:T(8,128)} %get-tuple-element.9, f32[2048,1]{1,0:T(8,128)S(1)} %copy.21), kind=kLoop, calls=%fused_computation.22 | loop fusion | flops 10240 | bytes 57344 | tf_op jit(solution)/shard_map/exp | solution.py:163
  144.3 7.5 %collective-permute-done.19 = f32[512,128]{1,0:T(8,128)S(1)} collective-permute-done((f32[512,128]{1,0:T(8,128)S(1)}, f32[512,128]{1,0:T(8,128)S(1)}, u32[]{:S(2)}, u32[]{:S(2)}) %collective-permute-start.19) | collective-permute-done | bytes 262176 | tf_op jit(solution)/shard_map/ppermute | solution.py:124
  (114 shorter events, 36.7 us)
Async XLA Ops:
  0.6 34.2 %copy-start.8 = (f32[2048,128]{1,0:T(8,128)S(1)}, f32[2048,128]{1,0:T(8,128)}, u32[]{:S(2)}) copy-start(f32[2048,128]{1,0:T(8,128)} %param.4) | copy-start | bytes 3145732
  0.6 22.8 %collective-permute-start.1 = (f32[512,128]{1,0:T(8,128)}, f32[512,128]{1,0:T(8,128)S(1)}, u32[]{:S(2)}, u32[]{:S(2)}) collective-permute-start(f32[512,128]{1,0:T(8,128)} %param.5), channel_id=1, source_target_pairs={{0,8},{4,12},{8,0},{12,4},{1,9},{5,13},{9,1},{13,5},{2,10},{6,14},... | collective-permute-start | bytes 786440 | tf_op jit(solution)/shard_map/ppermute | solution.py:137
  4.8 23.8 %collective-permute-start = (f32[512,128]{1,0:T(8,128)}, f32[512,128]{1,0:T(8,128)S(1)}, u32[]{:S(2)}, u32[]{:S(2)}) collective-permute-start(f32[512,128]{1,0:T(8,128)} %param.5), channel_id=1, source_target_pairs={{0,4},{4,8},{8,12},{12,0},{1,5},{5,9},{9,13},{13,1},{2,6},{6,10},{... | collective-permute-start | bytes 786440 | tf_op jit(solution)/shard_map/ppermute | solution.py:137
  6.3 28.3 %collective-permute-start.2 = (f32[512,128]{1,0:T(8,128)}, f32[512,128]{1,0:T(8,128)S(1)}, u32[]{:S(2)}, u32[]{:S(2)}) collective-permute-start(f32[512,128]{1,0:T(8,128)} %param.5), channel_id=1, source_target_pairs={{0,12},{4,0},{8,4},{12,8},{1,13},{5,1},{9,5},{13,9},{2,14},{6,2},{... | collective-permute-start | bytes 786440 | tf_op jit(solution)/shard_map/ppermute | solution.py:137
  16.4 40.9 %copy-start = (f32[2048,512]{1,0:T(8,128)}, f32[2048,512]{1,0:T(8,128)S(1)}, u32[]{:S(2)}) copy-start(f32[2048,512]{1,0:T(8,128)S(1)} %subtract_multiply_fusion.7) | copy-start | bytes 12582916
  28.5 28.7 %copy-start.2 = (f32[2048,512]{1,0:T(8,128)}, f32[2048,512]{1,0:T(8,128)S(1)}, u32[]{:S(2)}) copy-start(f32[2048,512]{1,0:T(8,128)S(1)} %subtract_multiply_fusion.5) | copy-start | bytes 12582916
  34.7 22.6 %copy-start.4 = (f32[2048,512]{1,0:T(8,128)}, f32[2048,512]{1,0:T(8,128)S(1)}, u32[]{:S(2)}) copy-start(f32[2048,512]{1,0:T(8,128)S(1)} %subtract_multiply_fusion.6) | copy-start | bytes 12582916
  49.9 3.3 %collective-permute-start.3 = (f32[2048]{0:T(1024)S(1)}, f32[2048]{0:T(1024)S(1)}, u32[]{:S(2)}, u32[]{:S(2)}) collective-permute-start(f32[2048]{0:T(1024)S(1)} %log_add_fusion.3), channel_id=1, source_target_pairs={{0,1},{1,2},{2,3},{3,0},{4,5},{5,6},{6,7},{7,4},{8,9},{9,10},{10,1... | collective-permute-start | bytes 24584 | tf_op jit(solution)/shard_map/ppermute | solution.py:98
  50.0 3.7 %collective-permute-start.4 = (f32[2048]{0:T(1024)S(1)}, f32[2048]{0:T(1024)S(1)}, u32[]{:S(2)}, u32[]{:S(2)}) collective-permute-start(f32[2048]{0:T(1024)S(1)} %log_add_fusion.3), channel_id=1, source_target_pairs={{0,2},{1,3},{2,0},{3,1},{4,6},{5,7},{6,4},{7,5},{8,10},{9,11},{10,... | collective-permute-start | bytes 24584 | tf_op jit(solution)/shard_map/ppermute | solution.py:98
  51.9 2.8 %collective-permute-start.5 = (f32[2048]{0:T(1024)S(1)}, f32[2048]{0:T(1024)S(1)}, u32[]{:S(2)}, u32[]{:S(2)}) collective-permute-start(f32[2048]{0:T(1024)S(1)} %log_add_fusion.3), channel_id=1, source_target_pairs={{0,3},{1,0},{2,1},{3,2},{4,7},{5,4},{6,5},{7,6},{8,11},{9,8},{10,9... | collective-permute-start | bytes 24584 | tf_op jit(solution)/shard_map/ppermute | solution.py:98
  62.4 5.4 %collective-permute-start.6 = (f32[2048]{0:T(1024)S(1)}, f32[2048]{0:T(1024)S(1)}, u32[]{:S(2)}, u32[]{:S(2)}) collective-permute-start(f32[2048]{0:T(1024)S(1)} %bitcast.85), channel_id=1, source_target_pairs={{0,4},{4,8},{8,12},{12,0},{1,5},{5,9},{9,13},{13,1},{2,6},{6,10},{... | collective-permute-start | bytes 24584 | tf_op jit(solution)/shard_map/ppermute | solution.py:98
  62.4 5.4 %collective-permute-start.7 = (f32[2048]{0:T(1024)S(1)}, f32[2048]{0:T(1024)S(1)}, u32[]{:S(2)}, u32[]{:S(2)}) collective-permute-start(f32[2048]{0:T(1024)S(1)} %bitcast.86), channel_id=1, source_target_pairs={{0,8},{4,12},{8,0},{12,4},{1,9},{5,13},{9,1},{13,5},{2,10},{6,14},... | collective-permute-start | bytes 24584 | tf_op jit(solution)/shard_map/ppermute | solution.py:98
  63.6 4.8 %collective-permute-start.8 = (f32[2048]{0:T(1024)S(1)}, f32[2048]{0:T(1024)S(1)}, u32[]{:S(2)}, u32[]{:S(2)}) collective-permute-start(f32[2048]{0:T(1024)S(1)} %bitcast.87), channel_id=1, source_target_pairs={{0,12},{4,0},{8,4},{12,8},{1,13},{5,1},{9,5},{13,9},{2,14},{6,2},{... | collective-permute-start | bytes 24584 | tf_op jit(solution)/shard_map/ppermute | solution.py:98
  84.5 3.7 %collective-permute-start.10 = (f32[2048]{0:T(1024)S(1)}, f32[2048]{0:T(1024)S(1)}, u32[]{:S(2)}, u32[]{:S(2)}) collective-permute-start(f32[2048]{0:T(1024)S(1)} %log_add_fusion.1), channel_id=1, source_target_pairs={{0,2},{1,3},{2,0},{3,1},{4,6},{5,7},{6,4},{7,5},{8,10},{9,11},{10,... | collective-permute-start | bytes 24584 | tf_op jit(solution)/shard_map/ppermute | solution.py:98
  85.5 2.7 %collective-permute-start.11 = (f32[2048]{0:T(1024)S(1)}, f32[2048]{0:T(1024)S(1)}, u32[]{:S(2)}, u32[]{:S(2)}) collective-permute-start(f32[2048]{0:T(1024)S(1)} %log_add_fusion.1), channel_id=1, source_target_pairs={{0,3},{1,0},{2,1},{3,2},{4,7},{5,4},{6,5},{7,6},{8,11},{9,8},{10,9... | collective-permute-start | bytes 24584 | tf_op jit(solution)/shard_map/ppermute | solution.py:98
  85.5 3.1 %collective-permute-start.9 = (f32[2048]{0:T(1024)S(1)}, f32[2048]{0:T(1024)S(1)}, u32[]{:S(2)}, u32[]{:S(2)}) collective-permute-start(f32[2048]{0:T(1024)S(1)} %log_add_fusion.1), channel_id=1, source_target_pairs={{0,1},{1,2},{2,3},{3,0},{4,5},{5,6},{6,7},{7,4},{8,9},{9,10},{10,1... | collective-permute-start | bytes 24584 | tf_op jit(solution)/shard_map/ppermute | solution.py:98
  96.5 5.4 %collective-permute-start.12 = (f32[2048]{0:T(1024)S(1)}, f32[2048]{0:T(1024)S(1)}, u32[]{:S(2)}, u32[]{:S(2)}) collective-permute-start(f32[2048]{0:T(1024)S(1)} %bitcast.81), channel_id=1, source_target_pairs={{0,4},{4,8},{8,12},{12,0},{1,5},{5,9},{9,13},{13,1},{2,6},{6,10},{... | collective-permute-start | bytes 24584 | tf_op jit(solution)/shard_map/ppermute | solution.py:98
  98.4 4.5 %collective-permute-start.13 = (f32[2048]{0:T(1024)S(1)}, f32[2048]{0:T(1024)S(1)}, u32[]{:S(2)}, u32[]{:S(2)}) collective-permute-start(f32[2048]{0:T(1024)S(1)} %bitcast.82), channel_id=1, source_target_pairs={{0,8},{4,12},{8,0},{12,4},{1,9},{5,13},{9,1},{13,5},{2,10},{6,14},... | collective-permute-start | bytes 24584 | tf_op jit(solution)/shard_map/ppermute | solution.py:98
  100.4 3.7 %collective-permute-start.14 = (f32[2048]{0:T(1024)S(1)}, f32[2048]{0:T(1024)S(1)}, u32[]{:S(2)}, u32[]{:S(2)}) collective-permute-start(f32[2048]{0:T(1024)S(1)} %bitcast.83), channel_id=1, source_target_pairs={{0,12},{4,0},{8,4},{12,8},{1,13},{5,1},{9,5},{13,9},{2,14},{6,2},{... | collective-permute-start | bytes 24584 | tf_op jit(solution)/shard_map/ppermute | solution.py:98
  129.4 3.1 %collective-permute-start.15 = (f32[2048]{0:T(1024)S(1)}, f32[2048]{0:T(1024)S(1)}, u32[]{:S(2)}, u32[]{:S(2)}) collective-permute-start(f32[2048]{0:T(1024)S(1)} %reduce.20), channel_id=1, source_target_pairs={{0,1},{1,2},{2,3},{3,0},{4,5},{5,6},{6,7},{7,4},{8,9},{9,10},{10,1... | collective-permute-start | bytes 24584 | tf_op jit(solution)/shard_map/ppermute | solution.py:98
  129.5 3.7 %collective-permute-start.16 = (f32[2048]{0:T(1024)S(1)}, f32[2048]{0:T(1024)S(1)}, u32[]{:S(2)}, u32[]{:S(2)}) collective-permute-start(f32[2048]{0:T(1024)S(1)} %reduce.20), channel_id=1, source_target_pairs={{0,2},{1,3},{2,0},{3,1},{4,6},{5,7},{6,4},{7,5},{8,10},{9,11},{10,... | collective-permute-start | bytes 24584 | tf_op jit(solution)/shard_map/ppermute | solution.py:98
  130.7 2.8 %collective-permute-start.17 = (f32[2048]{0:T(1024)S(1)}, f32[2048]{0:T(1024)S(1)}, u32[]{:S(2)}, u32[]{:S(2)}) collective-permute-start(f32[2048]{0:T(1024)S(1)} %reduce.20), channel_id=1, source_target_pairs={{0,3},{1,0},{2,1},{3,2},{4,7},{5,4},{6,5},{7,6},{8,11},{9,8},{10,9... | collective-permute-start | bytes 24584 | tf_op jit(solution)/shard_map/ppermute | solution.py:98
  140.5 2.6 %collective-permute-start.18 = (f32[2,512,128]{2,1,0:T(8,128)S(1)}, f32[2,512,128]{2,1,0:T(8,128)S(1)}, u32[]{:S(2)}, u32[]{:S(2)}) collective-permute-start(f32[2,512,128]{2,1,0:T(8,128)S(1)} %dynamic-slice_bitcast_fusion), channel_id=1, source_target_pairs={{0,1},{1,0},{2,3},{3,2},{4,5},{5,4},{6,7},{7,6},{8,9},{9,8},{10,11... | collective-permute-start | bytes 1572872 | tf_op jit(solution)/shard_map/ppermute | solution.py:119
  143.1 8.7 %collective-permute-start.19 = (f32[512,128]{1,0:T(8,128)S(1)}, f32[512,128]{1,0:T(8,128)S(1)}, u32[]{:S(2)}, u32[]{:S(2)}) collective-permute-start(f32[512,128]{1,0:T(8,128)S(1)} %dynamic-slice_bitcast_fusion.1), channel_id=1, source_target_pairs={{0,2},{1,3},{2,0},{3,1},{4,6},{5,7},{6,4},{7,5},{8,10},{9,11},{10,... | collective-permute-start | bytes 786440 | tf_op jit(solution)/shard_map/ppermute | solution.py:124
  (6 other events, 67.7 us)
where the time goes:
time: 153 us
  other arithmetic  50.2 us (33%)
  starting transfers between devices  26.1 us (17%)
  waiting for transfers between devices  25.5 us (17%)
  Pallas kernels  21.7 us (14%)
  matrix products  19.7 us (13%)
  local copies, waits for them, and re-layouts  8.27 us (5%)
    pallas_call x1, Pallas kernels, final_local(): pl.pallas_call(_final_kernel, grid=(R // tr,), in_specs=[pl.BlockSpec((1,...  21.7 us
    dot_general x4, matrix products, pair_cost(): lax.dot_general(block_rows, columns, (((1,), (1,)), ((), ())), precision=...  19.7 us
    ppermute x15, starting transfers between devices, lse_across(): lax.ppermute(local_lse, axis, shift_pairs(n, s))  15.9 us
    ppermute x15, waiting for transfers between devices, lse_across(): lax.ppermute(local_lse, axis, shift_pairs(n, s))  9.44 us
    reduce_sum x2, other arithmetic, on_device(): jnp.sum(jnp.exp(col_scores - col_peaks[None, :]), axis=0)  9.02 us
    reduce_sum x2, other arithmetic, row_lse(): local = peaks + jnp.log(jnp.sum(jnp.exp(scores - peaks[:, None]), axis=1))  8.78 us
    reduce_max x1, other arithmetic, row_lse(): peaks = jnp.max(scores, axis=1)  7.97 us
    ppermute x3, starting transfers between devices, on_device(): lax.ppermute(obs_days, 'mod', shift_pairs(n_mod, s))  7.95 us
  transfers between devices with their start and end apart: 20, of which 14 were waited for; matrix products, arithmetic and copies ran while one was open for 13% of the time, Pallas kernels for 0%

commit v1 on v0

--- a/solution.py
+++ b/solution.py
@@ -9,7 +9,6 @@
 
 ITERS = 2
 
-INV_E = 50.0
 RB = 8
 
 
@@ -19,7 +18,7 @@
 def _row_pass_max(h, c_ref, m_scr, tr):
     def p1(i, carry):
         r = pl.multiple_of(i * RB, RB)
-        tiles = _lane_tiles((h - c_ref[pl.ds(r, RB), :]) * INV_E)
+        tiles = _lane_tiles(h + c_ref[pl.ds(r, RB), :])
         m = tiles[0]
         for t in tiles[1:]:
             m = jnp.maximum(m, t)
@@ -36,7 +35,7 @@
     def p2(i, carry):
         r = pl.multiple_of(i * RB, RB)
         mr = m_ref[pl.ds(r, RB), :]
-        w = jnp.exp((h - c_ref[pl.ds(r, RB), :]) * INV_E - mr)
+        w = jnp.exp((h + c_ref[pl.ds(r, RB), :]) - mr)
         w_ref[pl.ds(r, RB), :] = w
         tiles = _lane_tiles(w)
         t = tiles[0]
@@ -81,7 +80,7 @@
     return [(i, (i + s) % n) for i in range(n)]
 
 
-def pair_cost(block_rows, block_square, columns):
+def pair_scores(block_rows, block_square, columns):
     column_square = jnp.sum(columns * columns, axis=1)
     cross = lax.dot_general(
         block_rows,
@@ -90,7 +89,8 @@
         precision=lax.Precision.HIGHEST,
         preferred_element_type=jnp.float32,
     )
-    return (block_square[:, None] + column_square[None, :] - 2.0 * cross) / block_rows.shape[1]
+    cost = (block_square[:, None] + column_square[None, :] - 2.0 * cross) / block_rows.shape[1]
+    return -cost / entropy_scale
 
 
 def lse_across(local_lse, axis):
@@ -138,12 +138,12 @@
     ]
     order = (m - jnp.arange(n_mod)) % n_mod
     gathered = jnp.concatenate(blocks, axis=0)
-    cost_tile = jnp.concatenate(
-        [pair_cost(model_days, row_square, b) for b in blocks], axis=1
+    base_tile = jnp.concatenate(
+        [pair_scores(model_days, row_square, b) for b in blocks], axis=1
     )
 
     def row_lse(col_potential):
-        scores = (col_potential[None, :] - cost_tile) / entropy_scale
+        scores = (col_potential / entropy_scale)[None, :] + base_tile
         peaks = jnp.max(scores, axis=1)
         local = peaks + jnp.log(jnp.sum(jnp.exp(scores - peaks[:, None]), axis=1))
         return lse_across(local, "obs")
@@ -151,13 +151,13 @@
     col_shift = jnp.zeros((col_count,), jnp.float32)
     for iteration in range(ITERS):
         row_potential = -entropy_scale * (row_lse(col_shift) - log_obs)
-        col_scores = (row_potential[:, None] - cost_tile) / entropy_scale
+        col_scores = (row_potential / entropy_scale)[:, None] + base_tile
         col_peaks = jnp.max(col_scores, axis=0)
         local = col_peaks + jnp.log(jnp.sum(jnp.exp(col_scores - col_peaks[None, :]), axis=0))
         col_global = lse_across(reorder(local, order), "mod")
         col_potential = -entropy_scale * (col_global - log_model)
         col_shift = reorder(col_potential, order)
-    peaks, local, partial_map = final_local(col_shift, cost_tile, gathered)
+    peaks, local, partial_map = final_local(col_shift / entropy_scale, base_tile, gathered)
     final_lse = lse_across(local, "obs")
     row_potential = -entropy_scale * (final_lse - log_obs)
     mapped = scatter_obs(partial_map * jnp.exp(peaks - final_lse)[:, None])

time: 153 us -> 144 us (0.941)
  other arithmetic: 50.2 us -> 41.7 us
  starting transfers between devices: 26.1 us -> 27.9 us
  matrix products: 19.7 us -> 18.1 us
    reduce_sum x2 -> x1, other arithmetic: 8.78 us -> 3.89 us  [row_lse(): local = peaks + jnp.log(jnp.sum(jnp.exp(scores - peaks[:, None]), axis=1))]
    ppermute x15, starting transfers between devices: 15.9 us -> 17.7 us  [lse_across(): lax.ppermute(local_lse, axis, shift_pairs(n, s))]
    reduce_sum x2, other arithmetic: 9.02 us -> 7.36 us  [on_device(): jnp.sum(jnp.exp(col_scores - col_peaks[None, :]), axis=0)]
    dot_general x4, matrix products: 19.7 us -> 18.1 us  [pair_scores(): lax.dot_general(block_rows, columns, (((1,), (1,)), ((), ())), precision=...]
    unnamed x26 -> x30, local copies, waits for them, and re-layouts: 3.38 us -> 3.71 us
    reduce_max x1 -> x2, other arithmetic: 7.97 us -> 7.73 us  [row_lse(): peaks = jnp.max(scores, axis=1)]
  transfers between devices with their start and end apart: 20 -> 20, of which waited for: 14 -> 13; matrix products, arithmetic and copies ran while one was open for 13% -> 13% of each run, Pallas kernels for 0% -> 0%
where the time goes in v1:
time: 144 us
  other arithmetic  41.7 us (29%)
  starting transfers between devices  27.9 us (19%)
  waiting for transfers between devices  24.7 us (17%)
  Pallas kernels  21.2 us (15%)
  matrix products  18.1 us (13%)
  local copies, waits for them, and re-layouts  9.64 us (7%)
    pallas_call x1, Pallas kernels, final_local(): pl.pallas_call(_final_kernel, grid=(R // tr,), in_specs=[pl.BlockSpec((1,...  21.2 us
    dot_general x4, matrix products, pair_scores(): lax.dot_general(block_rows, columns, (((1,), (1,)), ((), ())), precision=...  18.1 us
    ppermute x15, starting transfers between devices, lse_across(): lax.ppermute(local_lse, axis, shift_pairs(n, s))  17.7 us
    ppermute x15, waiting for transfers between devices, lse_across(): lax.ppermute(local_lse, axis, shift_pairs(n, s))  9.19 us
    ppermute x3, starting transfers between devices, on_device(): lax.ppermute(obs_days, 'mod', shift_pairs(n_mod, s))  7.95 us
    reduce_max x2, other arithmetic, row_lse(): peaks = jnp.max(scores, axis=1)  7.73 us
    ppermute x1, waiting for transfers between devices, scatter_obs(): total = total + lax.ppermute(piece, 'obs', pairs)  7.39 us
    reduce_sum x2, other arithmetic, on_device(): jnp.sum(jnp.exp(col_scores - col_peaks[None, :]), axis=0)  7.36 us
  transfers between devices with their start and end apart: 20, of which 13 were waited for; matrix products, arithmetic and copies ran while one was open for 13% of the time, Pallas kernels for 0%

profile of v1, /device:TPU:0, one launch (start us, length us, event | category | flops | bytes accessed | tf_op | source)
XLA Modules:
  0.0 144.2 jit_solution(14938415635485074233)
XLA Ops:
  0.6 4.1 %collective-permute-start.1 = (f32[512,128]{1,0:T(8,128)}, f32[512,128]{1,0:T(8,128)S(1)}, u32[]{:S(2)}, u32[]{:S(2)}) collective-permute-start(f32[512,128]{1,0:T(8,128)} %param.5), channel_id=1, source_target_pairs={{0,8},{4,12},{8,0},{12,4},{1,9},{5,13},{9,1},{13,5},{2,10},{6,14},... | collective-permute-start | bytes 786440 | tf_op jit(solution)/shard_map/ppermute | solution.py:137
  6.3 2.2 %collective-permute-start.2 = (f32[512,128]{1,0:T(8,128)}, f32[512,128]{1,0:T(8,128)S(1)}, u32[]{:S(2)}, u32[]{:S(2)}) collective-permute-start(f32[512,128]{1,0:T(8,128)} %param.5), channel_id=1, source_target_pairs={{0,12},{4,0},{8,4},{12,8},{1,13},{5,1},{9,5},{13,9},{2,14},{6,2},{... | collective-permute-start | bytes 786440 | tf_op jit(solution)/shard_map/ppermute | solution.py:137
  9.7 1.7 %multiply_reduce_fusion = f32[2048]{0:T(1024)S(1)} fusion(f32[2048,128]{1,0:T(8,128)} %param.4), kind=kLoop, calls=%fused_computation.18 | loop fusion | flops 522240 | bytes 1056768 | tf_op jit(solution)/shard_map/reduce_sum | solution.py:129
  11.4 5.4 %fusion.15 = (f32[2048]{0:T(1024)S(1)}, f32[2048,512]{1,0:T(8,128)S(1)}) fusion(f32[2048,128]{1,0:T(8,128)} %param.4, f32[512,128]{1,0:T(8,128)} %param.5, f32[512]{0:T(512)S(1)} %multiply_reduce_fusion.4, f32[2048]{0:T(1024)S(1)} %multiply_reduce_fusion), kind=kOutput, calls=%fused_computation.76 | convolution fusion | flops 1617950720 | bytes 5523456 | tf_op jit(solution)/shard_map/dot_general | solution.py:85
  16.9 6.5 %collective-permute-done.1 = f32[512,128]{1,0:T(8,128)S(1)} collective-permute-done((f32[512,128]{1,0:T(8,128)}, f32[512,128]{1,0:T(8,128)S(1)}, u32[]{:S(2)}, u32[]{:S(2)}) %collective-permute-start.1) | collective-permute-done | bytes 262176 | tf_op jit(solution)/shard_map/ppermute | solution.py:137
  23.6 4.2 %fusion.14 = (f32[2048]{0:T(1024)S(1)}, f32[2048,512]{1,0:T(8,128)S(1)}) fusion(f32[2048,128]{1,0:T(8,128)S(1)} %copy-done.9, f32[512,128]{1,0:T(8,128)S(1)} %collective-permute-done.1, f32[512]{0:T(512)S(1)} %multiply_reduce_fusion.2, f32[2048]{0:T(1024)S(1)} %multiply_reduce_fusion), kind=kOutput, calls=%fused_computation.75 | convolution fusion | flops 1617950720 | bytes 5523456 | tf_op jit(solution)/shard_map/dot_general | solution.py:85
  27.9 4.4 %fusion.16 = (f32[2048]{0:T(1024)S(1)}, f32[2048,512]{1,0:T(8,128)S(1)}) fusion(f32[2048,128]{1,0:T(8,128)S(1)} %copy-done.9, f32[512,128]{1,0:T(8,128)S(1)} %collective-permute-done, f32[512]{0:T(512)S(1)} %multiply_reduce_fusion.3, f32[2048]{0:T(1024)S(1)} %multiply_reduce_fusion), kind=kOutput, calls=%fused_computation.77 | convolution fusion | flops 1617950720 | bytes 5523456 | tf_op jit(solution)/shard_map/dot_general | solution.py:85
  32.4 4.2 %fusion.13 = (f32[2048]{0:T(1024)S(1)}, f32[2048,512]{1,0:T(8,128)S(1)}) fusion(f32[2048,128]{1,0:T(8,128)S(1)} %copy-done.9, f32[512,128]{1,0:T(8,128)S(1)} %collective-permute-done.2, f32[512]{0:T(512)S(1)} %multiply_reduce_fusion.1, f32[2048]{0:T(1024)S(1)} %multiply_reduce_fusion), kind=kOutput, calls=%fused_computation.74 | convolution fusion | flops 1617950720 | bytes 5523456 | tf_op jit(solution)/shard_map/dot_general | solution.py:85
  36.6 7.2 %pad_maximum_fusion = (f32[2048,2048]{1,0:T(8,128)}, f32[2048]{0:T(1024)S(1)}) fusion(f32[2048,512]{1,0:T(8,128)S(1)} %get-tuple-element.21, f32[2048,512]{1,0:T(8,128)S(1)} %get-tuple-element.23, f32[2048,512]{1,0:T(8,128)S(1)} %get-tuple-element.27, f32[2048,512]{1,0:T(8,128)S(1)} %get-tuple-element.25, f32[2048]{0:T(1024)S(1)} %maximum_maximum_fusion.5), kind=kLoop, calls=%fused_computation.4 | loop fusion | flops 20969472 | bytes 33570816 | tf_op jit(solution)/shard_map/concatenate | solution.py:141
  43.8 1.9 %collective-permute-start.4 = (f32[2048]{0:T(1024)S(1)}, f32[2048]{0:T(1024)S(1)}, u32[]{:S(2)}, u32[]{:S(2)}) collective-permute-start(f32[2048]{0:T(1024)S(1)} %log_add_fusion.3), channel_id=1, source_target_pairs={{0,2},{1,3},{2,0},{3,1},{4,6},{5,7},{6,4},{7,5},{8,10},{9,11},{10,... | collective-permute-start | bytes 24584 | tf_op jit(solution)/shard_map/ppermute | solution.py:98
  48.5 2.0 %add_reduce_fusion.2 = f32[2048]{0:T(1024)S(1)} fusion(f32[2048]{0:T(1024)S(1)} %add_multiply_fusion.5, f32[2048,512]{1,0:T(8,128)S(1)} %get-tuple-element.21, f32[2048,512]{1,0:T(8,128)S(1)} %get-tuple-element.23, f32[2048,512]{1,0:T(8,128)S(1)} %get-tuple-element.27, f32[2048,512]{1,0:T(8,128)S(1)} %get-tuple-element.25), kind=kLoop, calls=%fused_computation.11 | loop fusion | flops 20969472 | bytes 16793600 | tf_op jit(solution)/shard_map/reduce_max | solution.py:155
  50.6 3.7 %exponential_reduce_fusion.2 = f32[2048]{0:T(1024)S(1)} fusion(f32[2048]{0:T(1024)S(1)} %add_reduce_fusion.2, f32[2048]{0:T(1024)S(1)} %add_multiply_fusion.5, f32[2048,512]{1,0:T(8,128)S(1)} %get-tuple-element.21, f32[2048,512]{1,0:T(8,128)S(1)} %get-tuple-element.23, f32[2048,512]{1,0:T(8,128)S(1)} %get-tuple-element.27, f32[2048,512]{1,0:T(8,128)S(1)} %get-tuple-element.25), kind=kLoop, calls=%fused_computation.7 | loop fusion | flops 25163776 | bytes 16801792 | tf_op jit(solution)/shard_map/reduce_sum | solution.py:156
  55.8 1.9 %collective-permute-start.7 = (f32[2048]{0:T(1024)S(1)}, f32[2048]{0:T(1024)S(1)}, u32[]{:S(2)}, u32[]{:S(2)}) collective-permute-start(f32[2048]{0:T(1024)S(1)} %bitcast.86), channel_id=1, source_target_pairs={{0,8},{4,12},{8,0},{12,4},{1,9},{5,13},{9,1},{13,5},{2,10},{6,14},... | collective-permute-start | bytes 24584 | tf_op jit(solution)/shard_map/ppermute | solution.py:98
  57.7 2.9 %collective-permute-start.8 = (f32[2048]{0:T(1024)S(1)}, f32[2048]{0:T(1024)S(1)}, u32[]{:S(2)}, u32[]{:S(2)}) collective-permute-start(f32[2048]{0:T(1024)S(1)} %bitcast.87), channel_id=1, source_target_pairs={{0,12},{4,0},{8,4},{12,8},{1,13},{5,1},{9,5},{13,9},{2,14},{6,2},{... | collective-permute-start | bytes 24584 | tf_op jit(solution)/shard_map/ppermute | solution.py:98
  62.8 7.7 %add_reduce_fusion.1 = f32[2048]{0:T(1024)S(1)} fusion(f32[2048]{0:T(1024)S(1)} %bitcast.62, f32[2048,512]{1,0:T(8,128)} %copy-done.6, f32[2048,512]{1,0:T(8,128)} %copy-done.2, f32[2048,512]{1,0:T(8,128)} %copy-done.4, f32[2048,512]{1,0:T(8,128)} %copy-done), kind=kLoop, calls=%fused_computation.10 | loop fusion | flops 20969472 | bytes 16793600 | tf_op jit(solution)/shard_map/reduce_max | solution.py:147
  73.6 3.9 %exponential_reduce_fusion.1 = f32[2048]{0:T(1024)S(1)} fusion(f32[2048]{0:T(1024)S(1)} %add_reduce_fusion.1, f32[2048]{0:T(1024)S(1)} %bitcast.63, f32[2048,512]{1,0:T(8,128)S(1)} %copy-done.7, f32[2048,512]{1,0:T(8,128)S(1)} %copy-done.3, f32[2048,512]{1,0:T(8,128)S(1)} %copy-done.5, f32[2048,512]{1,0:T(8,128)S(1)} %copy-done.1), kind=kLoop, calls=%fused_computation.6 | loop fusion | flops 25163776 | bytes 16801792 | tf_op jit(solution)/shard_map/reduce_sum | solution.py:148
  79.0 2.2 %collective-permute-done.10 = f32[2048]{0:T(1024)S(1)} collective-permute-done((f32[2048]{0:T(1024)S(1)}, f32[2048]{0:T(1024)S(1)}, u32[]{:S(2)}, u32[]{:S(2)}) %collective-permute-start.10) | collective-permute-done | bytes 8224 | tf_op jit(solution)/shard_map/ppermute | solution.py:98
  81.6 2.0 %add_reduce_fusion = f32[2048]{0:T(1024)S(1)} fusion(f32[2048]{0:T(1024)S(1)} %add_multiply_fusion.3, f32[2048,512]{1,0:T(8,128)S(1)} %copy-done.7, f32[2048,512]{1,0:T(8,128)S(1)} %copy-done.3, f32[2048,512]{1,0:T(8,128)S(1)} %copy-done.5, f32[2048,512]{1,0:T(8,128)S(1)} %copy-done.1), kind=kLoop, calls=%fused_computation.9 | loop fusion | flops 20969472 | bytes 16793600 | tf_op jit(solution)/shard_map/reduce_max | solution.py:155
  83.6 3.7 %exponential_reduce_fusion = f32[2048]{0:T(1024)S(1)} fusion(f32[2048]{0:T(1024)S(1)} %add_reduce_fusion, f32[2048]{0:T(1024)S(1)} %add_multiply_fusion.3, f32[2048,512]{1,0:T(8,128)S(1)} %copy-done.7, f32[2048,512]{1,0:T(8,128)S(1)} %copy-done.3, f32[2048,512]{1,0:T(8,128)S(1)} %copy-done.5, f32[2048,512]{1,0:T(8,128)S(1)} %copy-done.1), kind=kLoop, calls=%fused_computation.5 | loop fusion | flops 25163776 | bytes 16801792 | tf_op jit(solution)/shard_map/reduce_sum | solution.py:156
  89.0 3.6 %collective-permute-start.13 = (f32[2048]{0:T(1024)S(1)}, f32[2048]{0:T(1024)S(1)}, u32[]{:S(2)}, u32[]{:S(2)}) collective-permute-start(f32[2048]{0:T(1024)S(1)} %bitcast.82), channel_id=1, source_target_pairs={{0,8},{4,12},{8,0},{12,4},{1,9},{5,13},{9,1},{13,5},{2,10},{6,14},... | collective-permute-start | bytes 24584 | tf_op jit(solution)/shard_map/ppermute | solution.py:98
  94.3 2.0 %collective-permute-done.14 = f32[2048]{0:T(1024)S(1)} collective-permute-done((f32[2048]{0:T(1024)S(1)}, f32[2048]{0:T(1024)S(1)}, u32[]{:S(2)}, u32[]{:S(2)}) %collective-permute-start.14) | collective-permute-done | bytes 8224 | tf_op jit(solution)/shard_map/ppermute | solution.py:98
  98.4 21.2 %shard_map.49 = (f32[2048,1]{1,0:T(8,128)}, f32[2048,1]{1,0:T(8,128)}, f32[2048,128]{1,0:T(8,128)}) custom-call(f32[1,2048]{1,0:T(1,128)} %bitcast.79, f32[2048,2048]{1,0:T(8,128)} %get-tuple-element.10.c_ref, f32[2048,128]{1,0:T(8,128)} %pad_maximum_fusion.1.y_ref), custom_call_target="tpu_custom_call" | custom-call | tf_op jit(solution)/shard_map/pallas_call | solution.py:62
  129.5 2.3 %exponential_reduce_fusion.4 = f32[2048]{0:T(1024)S(1)} fusion(f32[2048,1]{1,0:T(8,128)} %get-tuple-element.8, f32[2048,1]{1,0:T(8,128)S(1)} %copy.24, f32[2048,1]{1,0:T(8,128)} %copy.23, f32[2048,1]{1,0:T(8,128)} %copy.22, f32[2048,1]{1,0:T(8,128)S(1)} %copy-done.8, f32[2048,1]{1,0:T(8,128)S(1)} %copy.21), kind=kLoop, calls=%fused_computation.17 | loop fusion | flops 10240 | bytes 57344 | tf_op jit(solution)/shard_map/exp | solution.py:163
  136.1 7.4 %collective-permute-done.19 = f32[512,128]{1,0:T(8,128)S(1)} collective-permute-done((f32[512,128]{1,0:T(8,128)S(1)}, f32[512,128]{1,0:T(8,128)S(1)}, u32[]{:S(2)}, u32[]{:S(2)}) %collective-permute-start.19) | collective-permute-done | bytes 262176 | tf_op jit(solution)/shard_map/ppermute | solution.py:124
  (118 shorter events, 34.9 us)
Async XLA Ops:
  0.6 22.8 %collective-permute-start.1 = (f32[512,128]{1,0:T(8,128)}, f32[512,128]{1,0:T(8,128)S(1)}, u32[]{:S(2)}, u32[]{:S(2)}) collective-permute-start(f32[512,128]{1,0:T(8,128)} %param.5), channel_id=1, source_target_pairs={{0,8},{4,12},{8,0},{12,4},{1,9},{5,13},{9,1},{13,5},{2,10},{6,14},... | collective-permute-start | bytes 786440 | tf_op jit(solution)/shard_map/ppermute | solution.py:137
  4.8 23.0 %collective-permute-start = (f32[512,128]{1,0:T(8,128)}, f32[512,128]{1,0:T(8,128)S(1)}, u32[]{:S(2)}, u32[]{:S(2)}) collective-permute-start(f32[512,128]{1,0:T(8,128)} %param.5), channel_id=1, source_target_pairs={{0,4},{4,8},{8,12},{12,0},{1,5},{5,9},{9,13},{13,1},{2,6},{6,10},{... | collective-permute-start | bytes 786440 | tf_op jit(solution)/shard_map/ppermute | solution.py:137
  6.3 25.9 %collective-permute-start.2 = (f32[512,128]{1,0:T(8,128)}, f32[512,128]{1,0:T(8,128)S(1)}, u32[]{:S(2)}, u32[]{:S(2)}) collective-permute-start(f32[512,128]{1,0:T(8,128)} %param.5), channel_id=1, source_target_pairs={{0,12},{4,0},{8,4},{12,8},{1,13},{5,1},{9,5},{13,9},{2,14},{6,2},{... | collective-permute-start | bytes 786440 | tf_op jit(solution)/shard_map/ppermute | solution.py:137
  16.9 33.7 %copy-start = (f32[2048,512]{1,0:T(8,128)}, f32[2048,512]{1,0:T(8,128)S(1)}, u32[]{:S(2)}) copy-start(f32[2048,512]{1,0:T(8,128)S(1)} %get-tuple-element.25) | copy-start | bytes 12582916
  27.7 22.8 %copy-start.2 = (f32[2048,512]{1,0:T(8,128)}, f32[2048,512]{1,0:T(8,128)S(1)}, u32[]{:S(2)}) copy-start(f32[2048,512]{1,0:T(8,128)S(1)} %get-tuple-element.23) | copy-start | bytes 12582916
  32.2 18.3 %copy-start.4 = (f32[2048,512]{1,0:T(8,128)}, f32[2048,512]{1,0:T(8,128)S(1)}, u32[]{:S(2)}) copy-start(f32[2048,512]{1,0:T(8,128)S(1)} %get-tuple-element.27) | copy-start | bytes 12582916
  36.6 14.0 %copy-start.6 = (f32[2048,512]{1,0:T(8,128)}, f32[2048,512]{1,0:T(8,128)S(1)}, u32[]{:S(2)}) copy-start(f32[2048,512]{1,0:T(8,128)S(1)} %get-tuple-element.21) | copy-start | bytes 12582916
  43.8 3.3 %collective-permute-start.3 = (f32[2048]{0:T(1024)S(1)}, f32[2048]{0:T(1024)S(1)}, u32[]{:S(2)}, u32[]{:S(2)}) collective-permute-start(f32[2048]{0:T(1024)S(1)} %log_add_fusion.3), channel_id=1, source_target_pairs={{0,1},{1,2},{2,3},{3,0},{4,5},{5,6},{6,7},{7,4},{8,9},{9,10},{10,1... | collective-permute-start | bytes 24584 | tf_op jit(solution)/shard_map/ppermute | solution.py:98
  43.8 3.7 %collective-permute-start.4 = (f32[2048]{0:T(1024)S(1)}, f32[2048]{0:T(1024)S(1)}, u32[]{:S(2)}, u32[]{:S(2)}) collective-permute-start(f32[2048]{0:T(1024)S(1)} %log_add_fusion.3), channel_id=1, source_target_pairs={{0,2},{1,3},{2,0},{3,1},{4,6},{5,7},{6,4},{7,5},{8,10},{9,11},{10,... | collective-permute-start | bytes 24584 | tf_op jit(solution)/shard_map/ppermute | solution.py:98
  45.7 2.8 %collective-permute-start.5 = (f32[2048]{0:T(1024)S(1)}, f32[2048]{0:T(1024)S(1)}, u32[]{:S(2)}, u32[]{:S(2)}) collective-permute-start(f32[2048]{0:T(1024)S(1)} %log_add_fusion.3), channel_id=1, source_target_pairs={{0,3},{1,0},{2,1},{3,2},{4,7},{5,4},{6,5},{7,6},{8,11},{9,8},{10,9... | collective-permute-start | bytes 24584 | tf_op jit(solution)/shard_map/ppermute | solution.py:98
  54.9 5.7 %collective-permute-start.6 = (f32[2048]{0:T(1024)S(1)}, f32[2048]{0:T(1024)S(1)}, u32[]{:S(2)}, u32[]{:S(2)}) collective-permute-start(f32[2048]{0:T(1024)S(1)} %bitcast.85), channel_id=1, source_target_pairs={{0,4},{4,8},{8,12},{12,0},{1,5},{5,9},{9,13},{13,1},{2,6},{6,10},{... | collective-permute-start | bytes 24584 | tf_op jit(solution)/shard_map/ppermute | solution.py:98
  55.8 4.8 %collective-permute-start.7 = (f32[2048]{0:T(1024)S(1)}, f32[2048]{0:T(1024)S(1)}, u32[]{:S(2)}, u32[]{:S(2)}) collective-permute-start(f32[2048]{0:T(1024)S(1)} %bitcast.86), channel_id=1, source_target_pairs={{0,8},{4,12},{8,0},{12,4},{1,9},{5,13},{9,1},{13,5},{2,10},{6,14},... | collective-permute-start | bytes 24584 | tf_op jit(solution)/shard_map/ppermute | solution.py:98
  57.7 4.2 %collective-permute-start.8 = (f32[2048]{0:T(1024)S(1)}, f32[2048]{0:T(1024)S(1)}, u32[]{:S(2)}, u32[]{:S(2)}) collective-permute-start(f32[2048]{0:T(1024)S(1)} %bitcast.87), channel_id=1, source_target_pairs={{0,12},{4,0},{8,4},{12,8},{1,13},{5,1},{9,5},{13,9},{2,14},{6,2},{... | collective-permute-start | bytes 24584 | tf_op jit(solution)/shard_map/ppermute | solution.py:98
  77.5 3.7 %collective-permute-start.10 = (f32[2048]{0:T(1024)S(1)}, f32[2048]{0:T(1024)S(1)}, u32[]{:S(2)}, u32[]{:S(2)}) collective-permute-start(f32[2048]{0:T(1024)S(1)} %log_add_fusion.1), channel_id=1, source_target_pairs={{0,2},{1,3},{2,0},{3,1},{4,6},{5,7},{6,4},{7,5},{8,10},{9,11},{10,... | collective-permute-start | bytes 24584 | tf_op jit(solution)/shard_map/ppermute | solution.py:98
  78.5 2.8 %collective-permute-start.11 = (f32[2048]{0:T(1024)S(1)}, f32[2048]{0:T(1024)S(1)}, u32[]{:S(2)}, u32[]{:S(2)}) collective-permute-start(f32[2048]{0:T(1024)S(1)} %log_add_fusion.1), channel_id=1, source_target_pairs={{0,3},{1,0},{2,1},{3,2},{4,7},{5,4},{6,5},{7,6},{8,11},{9,8},{10,9... | collective-permute-start | bytes 24584 | tf_op jit(solution)/shard_map/ppermute | solution.py:98
  78.5 3.1 %collective-permute-start.9 = (f32[2048]{0:T(1024)S(1)}, f32[2048]{0:T(1024)S(1)}, u32[]{:S(2)}, u32[]{:S(2)}) collective-permute-start(f32[2048]{0:T(1024)S(1)} %log_add_fusion.1), channel_id=1, source_target_pairs={{0,1},{1,2},{2,3},{3,0},{4,5},{5,6},{6,7},{7,4},{8,9},{9,10},{10,1... | collective-permute-start | bytes 24584 | tf_op jit(solution)/shard_map/ppermute | solution.py:98
  88.0 5.7 %collective-permute-start.12 = (f32[2048]{0:T(1024)S(1)}, f32[2048]{0:T(1024)S(1)}, u32[]{:S(2)}, u32[]{:S(2)}) collective-permute-start(f32[2048]{0:T(1024)S(1)} %bitcast.81), channel_id=1, source_target_pairs={{0,4},{4,8},{8,12},{12,0},{1,5},{5,9},{9,13},{13,1},{2,6},{6,10},{... | collective-permute-start | bytes 24584 | tf_op jit(solution)/shard_map/ppermute | solution.py:98
  89.0 5.2 %collective-permute-start.13 = (f32[2048]{0:T(1024)S(1)}, f32[2048]{0:T(1024)S(1)}, u32[]{:S(2)}, u32[]{:S(2)}) collective-permute-start(f32[2048]{0:T(1024)S(1)} %bitcast.82), channel_id=1, source_target_pairs={{0,8},{4,12},{8,0},{12,4},{1,9},{5,13},{9,1},{13,5},{2,10},{6,14},... | collective-permute-start | bytes 24584 | tf_op jit(solution)/shard_map/ppermute | solution.py:98
  92.7 3.7 %collective-permute-start.14 = (f32[2048]{0:T(1024)S(1)}, f32[2048]{0:T(1024)S(1)}, u32[]{:S(2)}, u32[]{:S(2)}) collective-permute-start(f32[2048]{0:T(1024)S(1)} %bitcast.83), channel_id=1, source_target_pairs={{0,12},{4,0},{8,4},{12,8},{1,13},{5,1},{9,5},{13,9},{2,14},{6,2},{... | collective-permute-start | bytes 24584 | tf_op jit(solution)/shard_map/ppermute | solution.py:98
  121.2 3.1 %collective-permute-start.15 = (f32[2048]{0:T(1024)S(1)}, f32[2048]{0:T(1024)S(1)}, u32[]{:S(2)}, u32[]{:S(2)}) collective-permute-start(f32[2048]{0:T(1024)S(1)} %reduce.24), channel_id=1, source_target_pairs={{0,1},{1,2},{2,3},{3,0},{4,5},{5,6},{6,7},{7,4},{8,9},{9,10},{10,1... | collective-permute-start | bytes 24584 | tf_op jit(solution)/shard_map/ppermute | solution.py:98
  121.2 3.7 %collective-permute-start.16 = (f32[2048]{0:T(1024)S(1)}, f32[2048]{0:T(1024)S(1)}, u32[]{:S(2)}, u32[]{:S(2)}) collective-permute-start(f32[2048]{0:T(1024)S(1)} %reduce.24), channel_id=1, source_target_pairs={{0,2},{1,3},{2,0},{3,1},{4,6},{5,7},{6,4},{7,5},{8,10},{9,11},{10,... | collective-permute-start | bytes 24584 | tf_op jit(solution)/shard_map/ppermute | solution.py:98
  122.5 2.8 %collective-permute-start.17 = (f32[2048]{0:T(1024)S(1)}, f32[2048]{0:T(1024)S(1)}, u32[]{:S(2)}, u32[]{:S(2)}) collective-permute-start(f32[2048]{0:T(1024)S(1)} %reduce.24), channel_id=1, source_target_pairs={{0,3},{1,0},{2,1},{3,2},{4,7},{5,4},{6,5},{7,6},{8,11},{9,8},{10,9... | collective-permute-start | bytes 24584 | tf_op jit(solution)/shard_map/ppermute | solution.py:98
  132.2 2.5 %collective-permute-start.18 = (f32[2,512,128]{2,1,0:T(8,128)S(1)}, f32[2,512,128]{2,1,0:T(8,128)S(1)}, u32[]{:S(2)}, u32[]{:S(2)}) collective-permute-start(f32[2,512,128]{2,1,0:T(8,128)S(1)} %dynamic-slice_bitcast_fusion), channel_id=1, source_target_pairs={{0,1},{1,0},{2,3},{3,2},{4,5},{5,4},{6,7},{7,6},{8,9},{9,8},{10,11... | collective-permute-start | bytes 1572872 | tf_op jit(solution)/shard_map/ppermute | solution.py:119
  134.8 8.7 %collective-permute-start.19 = (f32[512,128]{1,0:T(8,128)S(1)}, f32[512,128]{1,0:T(8,128)S(1)}, u32[]{:S(2)}, u32[]{:S(2)}) collective-permute-start(f32[512,128]{1,0:T(8,128)S(1)} %dynamic-slice_bitcast_fusion.1), channel_id=1, source_target_pairs={{0,2},{1,3},{2,0},{3,1},{4,6},{5,7},{6,4},{7,5},{8,10},{9,11},{10,... | collective-permute-start | bytes 786440 | tf_op jit(solution)/shard_map/ppermute | solution.py:124
  (8 other events, 71.7 us)

commit v2 on v1

--- a/solution.py
+++ b/solution.py
@@ -106,7 +106,7 @@
     return jnp.take(vec.reshape(n, -1), order, axis=0).reshape(-1)
 
 
-def scatter_obs(partial):
+def scatter_obs(partial, peaks, final_lse):
     n = lax.axis_size("obs")
     half = n // 2
     o = lax.axis_index("obs")
@@ -114,14 +114,29 @@
     c = o % 2
     share = partial.shape[0] // n
     p4 = partial.reshape(half, 2, share, partial.shape[1])
+    m4 = peaks.reshape(half, 2, share)
     keep = lax.dynamic_index_in_dim(p4, c, axis=1, keepdims=False)
     give = lax.dynamic_index_in_dim(p4, 1 - c, axis=1, keepdims=False)
-    acc = keep + lax.ppermute(give, "obs", [(i, i ^ 1) for i in range(n)])
-    total = lax.dynamic_index_in_dim(acc, x, axis=0, keepdims=False)
+    m_keep = lax.dynamic_index_in_dim(m4, c, axis=1, keepdims=False)
+    m_give = lax.dynamic_index_in_dim(m4, 1 - c, axis=1, keepdims=False)
+    partner = [(i, i ^ 1) for i in range(n)]
+    got = lax.ppermute(give, "obs", partner)
+    m_got = lax.ppermute(m_give, "obs", partner)
+    top = jnp.maximum(m_keep, m_got)
+    acc = keep * jnp.exp(m_keep - top)[..., None] + got * jnp.exp(m_got - top)[..., None]
+    pieces = [(lax.dynamic_index_in_dim(acc, x, axis=0, keepdims=False),
+               lax.dynamic_index_in_dim(top, x, axis=0, keepdims=False))]
     for k in range(1, half):
         pairs = [(i, ((i // 2 + k) % half) * 2 + i % 2) for i in range(n)]
-        piece = lax.dynamic_index_in_dim(acc, (x + k) % half, axis=0, keepdims=False)
-        total = total + lax.ppermute(piece, "obs", pairs)
+        j = (x + k) % half
+        pieces.append((
+            lax.ppermute(lax.dynamic_index_in_dim(acc, j, axis=0, keepdims=False), "obs", pairs),
+            lax.ppermute(lax.dynamic_index_in_dim(top, j, axis=0, keepdims=False), "obs", pairs),
+        ))
+    own_lse = lax.dynamic_slice_in_dim(final_lse, o * share, share)
+    total = pieces[0][0] * jnp.exp(pieces[0][1] - own_lse)[:, None]
+    for piece, piece_top in pieces[1:]:
+        total = total + piece * jnp.exp(piece_top - own_lse)[:, None]
     return total
 
 
@@ -160,7 +175,7 @@
     peaks, local, partial_map = final_local(col_shift / entropy_scale, base_tile, gathered)
     final_lse = lse_across(local, "obs")
     row_potential = -entropy_scale * (final_lse - log_obs)
-    mapped = scatter_obs(partial_map * jnp.exp(peaks - final_lse)[:, None])
+    mapped = scatter_obs(partial_map, peaks, final_lse)
     return (mapped, row_potential, col_potential)
 
 

time: 144 us -> 149 us (1.035)
  other arithmetic: 41.7 us -> 47.8 us
  waiting for transfers between devices: 24.7 us -> 22 us
    reduce_max x2, other arithmetic: 4 us -> 9.81 us  [on_device(): col_peaks = jnp.max(col_scores, axis=0)]
    reduce_max x9 -> x6, local copies, waits for them, and re-layouts: 3.2 us -> 0.05 us  [lse_across(): top = jnp.max(stacked, axis=0)]
    unnamed x30 -> x35, local copies, waits for them, and re-layouts: 3.71 us -> 6.62 us
    exp x1, other arithmetic: 2.34 us -> 0.08 us  [scatter_obs(): total = pieces[0][0] * jnp.exp(pieces[0][1] - own_lse)[:, None]]
    add x2, other arithmetic: 0.79 us -> 2.28 us  [the longest x1 1.37 us: scatter_obs(): keep * jnp.exp(m_keep - top)[..., None]]
    pallas_call x1 -> x2, other arithmetic: 1.65 us -> 3.12 us  [final_local(): pl.pallas_call(_final_kernel, grid=(R // tr,), in_specs=[pl.BlockSpec((1,...]
    ppermute x2 -> x4, waiting for transfers between devices: 8.92 us -> 7.58 us  [the longest x1 7.06 us: scatter_obs(): lax.ppermute(lax.dynamic_index_in_dim(acc, j, axis=0, keepdims=False), 'o...]
  transfers between devices with their start and end apart: 20 -> 22, of which waited for: 13 -> 10; matrix products, arithmetic and copies ran while one was open for 13% -> 15% of each run, Pallas kernels for 0% -> 0%
where the time goes in v2:
time: 149 us; the launch traced here: 148 us
  other arithmetic  47.8 us (32%)
  starting transfers between devices  28.1 us (19%)
  waiting for transfers between devices  22 us (15%)
  Pallas kernels  21.2 us (14%)
  matrix products  18.1 us (12%)
  local copies, waits for them, and re-layouts  10.1 us (7%)
    pallas_call x1, Pallas kernels, final_local(): pl.pallas_call(_final_kernel, grid=(R // tr,), in_specs=[pl.BlockSpec((1,...  21.2 us
    dot_general x4, matrix products, pair_scores(): lax.dot_general(block_rows, columns, (((1,), (1,)), ((), ())), precision=...  18.1 us
    ppermute x15, starting transfers between devices, lse_across(): lax.ppermute(local_lse, axis, shift_pairs(n, s))  17.7 us
    reduce_max x2, other arithmetic, on_device(): col_peaks = jnp.max(col_scores, axis=0)  9.81 us
    ppermute x3, starting transfers between devices, on_device(): lax.ppermute(obs_days, 'mod', shift_pairs(n_mod, s))  7.95 us
    ppermute x15, waiting for transfers between devices, lse_across(): lax.ppermute(local_lse, axis, shift_pairs(n, s))  7.82 us
    reduce_max x2, other arithmetic, row_lse(): peaks = jnp.max(scores, axis=1)  7.73 us
    reduce_sum x2, other arithmetic, on_device(): jnp.sum(jnp.exp(col_scores - col_peaks[None, :]), axis=0)  7.32 us
  transfers between devices with their start and end apart: 22, of which 10 were waited for; matrix products, arithmetic and copies ran while one was open for 15% of the time, Pallas kernels for 0%

profile of v2, /device:TPU:0, one launch (start us, length us, event | category | flops | bytes accessed | tf_op | source)
XLA Modules:
  0.0 148.4 jit_solution(7616027569302764105)
XLA Ops:
  0.6 4.1 %collective-permute-start.1 = (f32[512,128]{1,0:T(8,128)}, f32[512,128]{1,0:T(8,128)S(1)}, u32[]{:S(2)}, u32[]{:S(2)}) collective-permute-start(f32[512,128]{1,0:T(8,128)} %param.5), channel_id=1, source_target_pairs={{0,8},{4,12},{8,0},{12,4},{1,9},{5,13},{9,1},{13,5},{2,10},{6,14},... | collective-permute-start | bytes 786440 | tf_op jit(solution)/shard_map/ppermute | solution.py:152
  4.8 1.6 %collective-permute-start = (f32[512,128]{1,0:T(8,128)}, f32[512,128]{1,0:T(8,128)S(1)}, u32[]{:S(2)}, u32[]{:S(2)}) collective-permute-start(f32[512,128]{1,0:T(8,128)} %param.5), channel_id=1, source_target_pairs={{0,4},{4,8},{8,12},{12,0},{1,5},{5,9},{9,13},{13,1},{2,6},{6,10},{... | collective-permute-start | bytes 786440 | tf_op jit(solution)/shard_map/ppermute | solution.py:152
  6.3 2.2 %collective-permute-start.2 = (f32[512,128]{1,0:T(8,128)}, f32[512,128]{1,0:T(8,128)S(1)}, u32[]{:S(2)}, u32[]{:S(2)}) collective-permute-start(f32[512,128]{1,0:T(8,128)} %param.5), channel_id=1, source_target_pairs={{0,12},{4,0},{8,4},{12,8},{1,13},{5,1},{9,5},{13,9},{2,14},{6,2},{... | collective-permute-start | bytes 786440 | tf_op jit(solution)/shard_map/ppermute | solution.py:152
  9.7 1.7 %multiply_reduce_fusion = f32[2048]{0:T(1024)S(1)} fusion(f32[2048,128]{1,0:T(8,128)} %param.4), kind=kLoop, calls=%fused_computation.17 | loop fusion | flops 522240 | bytes 1056768 | tf_op jit(solution)/shard_map/reduce_sum | solution.py:144
  11.4 5.4 %fusion.18 = (f32[2048]{0:T(1024)S(1)}, f32[2048,512]{1,0:T(8,128)S(1)}) fusion(f32[2048,128]{1,0:T(8,128)} %param.4, f32[512,128]{1,0:T(8,128)} %param.5, f32[512]{0:T(512)S(1)} %multiply_reduce_fusion.4, f32[2048]{0:T(1024)S(1)} %multiply_reduce_fusion), kind=kOutput, calls=%fused_computation.88 | convolution fusion | flops 1617950720 | bytes 5523456 | tf_op jit(solution)/shard_map/dot_general | solution.py:85
  16.9 6.5 %collective-permute-done.1 = f32[512,128]{1,0:T(8,128)S(1)} collective-permute-done((f32[512,128]{1,0:T(8,128)}, f32[512,128]{1,0:T(8,128)S(1)}, u32[]{:S(2)}, u32[]{:S(2)}) %collective-permute-start.1) | collective-permute-done | bytes 262176 | tf_op jit(solution)/shard_map/ppermute | solution.py:152
  23.6 4.2 %fusion.17 = (f32[2048]{0:T(1024)S(1)}, f32[2048,512]{1,0:T(8,128)S(1)}) fusion(f32[2048,128]{1,0:T(8,128)S(1)} %copy-done.12, f32[512,128]{1,0:T(8,128)S(1)} %collective-permute-done.1, f32[512]{0:T(512)S(1)} %multiply_reduce_fusion.2, f32[2048]{0:T(1024)S(1)} %multiply_reduce_fusion), kind=kOutput, calls=%fused_computation.87 | convolution fusion | flops 1617950720 | bytes 5523456 | tf_op jit(solution)/shard_map/dot_general | solution.py:85
  27.9 4.4 %fusion.19 = (f32[2048]{0:T(1024)S(1)}, f32[2048,512]{1,0:T(8,128)S(1)}) fusion(f32[2048,128]{1,0:T(8,128)S(1)} %copy-done.12, f32[512,128]{1,0:T(8,128)S(1)} %collective-permute-done, f32[512]{0:T(512)S(1)} %multiply_reduce_fusion.3, f32[2048]{0:T(1024)S(1)} %multiply_reduce_fusion), kind=kOutput, calls=%fused_computation.89 | convolution fusion | flops 1617950720 | bytes 5523456 | tf_op jit(solution)/shard_map/dot_general | solution.py:85
  32.4 4.2 %fusion.16 = (f32[2048]{0:T(1024)S(1)}, f32[2048,512]{1,0:T(8,128)S(1)}) fusion(f32[2048,128]{1,0:T(8,128)S(1)} %copy-done.12, f32[512,128]{1,0:T(8,128)S(1)} %collective-permute-done.2, f32[512]{0:T(512)S(1)} %multiply_reduce_fusion.1, f32[2048]{0:T(1024)S(1)} %multiply_reduce_fusion), kind=kOutput, calls=%fused_computation.86 | convolution fusion | flops 1617950720 | bytes 5523456 | tf_op jit(solution)/shard_map/dot_general | solution.py:85
  36.6 7.2 %pad_maximum_fusion = (f32[2048,2048]{1,0:T(8,128)}, f32[2048]{0:T(1024)S(1)}) fusion(f32[2048,512]{1,0:T(8,128)S(1)} %get-tuple-element.30, f32[2048,512]{1,0:T(8,128)S(1)} %get-tuple-element.32, f32[2048,512]{1,0:T(8,128)S(1)} %get-tuple-element.36, f32[2048,512]{1,0:T(8,128)S(1)} %get-tuple-element.34, f32[2048]{0:T(1024)S(1)} %maximum_maximum_fusion.5), kind=kLoop, calls=%fused_computation.4 | loop fusion | flops 20969472 | bytes 33570816 | tf_op jit(solution)/shard_map/concatenate | solution.py:156
  43.8 1.9 %collective-permute-start.4 = (f32[2048]{0:T(1024)S(1)}, f32[2048]{0:T(1024)S(1)}, u32[]{:S(2)}, u32[]{:S(2)}) collective-permute-start(f32[2048]{0:T(1024)S(1)} %log_add_fusion.4), channel_id=1, source_target_pairs={{0,2},{1,3},{2,0},{3,1},{4,6},{5,7},{6,4},{7,5},{8,10},{9,11},{10,... | collective-permute-start | bytes 24584 | tf_op jit(solution)/shard_map/ppermute | solution.py:98
  48.5 2.0 %add_reduce_fusion.2 = f32[2048]{0:T(1024)S(1)} fusion(f32[2048]{0:T(1024)S(1)} %add_multiply_fusion.5, f32[2048,512]{1,0:T(8,128)S(1)} %get-tuple-element.30, f32[2048,512]{1,0:T(8,128)S(1)} %get-tuple-element.32, f32[2048,512]{1,0:T(8,128)S(1)} %get-tuple-element.36, f32[2048,512]{1,0:T(8,128)S(1)} %get-tuple-element.34), kind=kLoop, calls=%fused_computation.11 | loop fusion | flops 20969472 | bytes 16793600 | tf_op jit(solution)/shard_map/reduce_max | solution.py:170
  50.6 3.7 %exponential_reduce_fusion.2 = f32[2048]{0:T(1024)S(1)} fusion(f32[2048]{0:T(1024)S(1)} %add_reduce_fusion.2, f32[2048]{0:T(1024)S(1)} %add_multiply_fusion.5, f32[2048,512]{1,0:T(8,128)S(1)} %get-tuple-element.30, f32[2048,512]{1,0:T(8,128)S(1)} %get-tuple-element.32, f32[2048,512]{1,0:T(8,128)S(1)} %get-tuple-element.36, f32[2048,512]{1,0:T(8,128)S(1)} %get-tuple-element.34), kind=kLoop, calls=%fused_computation.7 | loop fusion | flops 25163776 | bytes 16801792 | tf_op jit(solution)/shard_map/reduce_sum | solution.py:171
  55.8 1.9 %collective-permute-start.7 = (f32[2048]{0:T(1024)S(1)}, f32[2048]{0:T(1024)S(1)}, u32[]{:S(2)}, u32[]{:S(2)}) collective-permute-start(f32[2048]{0:T(1024)S(1)} %bitcast.93), channel_id=1, source_target_pairs={{0,8},{4,12},{8,0},{12,4},{1,9},{5,13},{9,1},{13,5},{2,10},{6,14},... | collective-permute-start | bytes 24584 | tf_op jit(solution)/shard_map/ppermute | solution.py:98
  57.7 2.9 %collective-permute-start.8 = (f32[2048]{0:T(1024)S(1)}, f32[2048]{0:T(1024)S(1)}, u32[]{:S(2)}, u32[]{:S(2)}) collective-permute-start(f32[2048]{0:T(1024)S(1)} %bitcast.94), channel_id=1, source_target_pairs={{0,12},{4,0},{8,4},{12,8},{1,13},{5,1},{9,5},{13,9},{2,14},{6,2},{... | collective-permute-start | bytes 24584 | tf_op jit(solution)/shard_map/ppermute | solution.py:98
  62.8 7.7 %add_reduce_fusion.1 = f32[2048]{0:T(1024)S(1)} fusion(f32[2048]{0:T(1024)S(1)} %bitcast.76, f32[2048,512]{1,0:T(8,128)} %copy-done.9, f32[2048,512]{1,0:T(8,128)} %copy-done.3, f32[2048,512]{1,0:T(8,128)} %copy-done.6, f32[2048,512]{1,0:T(8,128)} %copy-done), kind=kLoop, calls=%fused_computation.10 | loop fusion | flops 20969472 | bytes 16793600 | tf_op jit(solution)/shard_map/reduce_max | solution.py:162
  73.6 3.9 %exponential_reduce_fusion.1 = f32[2048]{0:T(1024)S(1)} fusion(f32[2048]{0:T(1024)S(1)} %add_reduce_fusion.1, f32[2048]{0:T(1024)S(1)} %bitcast.77, f32[2048,512]{1,0:T(8,128)S(1)} %copy-done.10, f32[2048,512]{1,0:T(8,128)S(1)} %copy-done.4, f32[2048,512]{1,0:T(8,128)S(1)} %copy-done.7, f32[2048,512]{1,0:T(8,128)S(1)} %copy-done.1), kind=kLoop, calls=%fused_computation.6 | loop fusion | flops 25163776 | bytes 16801792 | tf_op jit(solution)/shard_map/reduce_sum | solution.py:163
  79.0 2.2 %collective-permute-done.10 = f32[2048]{0:T(1024)S(1)} collective-permute-done((f32[2048]{0:T(1024)S(1)}, f32[2048]{0:T(1024)S(1)}, u32[]{:S(2)}, u32[]{:S(2)}) %collective-permute-start.10) | collective-permute-done | bytes 8224 | tf_op jit(solution)/shard_map/ppermute | solution.py:98
  81.7 7.8 %add_reduce_fusion = f32[2048]{0:T(1024)S(1)} fusion(f32[2048]{0:T(1024)S(1)} %add_multiply_fusion.3, f32[2048,512]{1,0:T(8,128)} %copy-done.9, f32[2048,512]{1,0:T(8,128)} %copy-done.3, f32[2048,512]{1,0:T(8,128)} %copy-done.6, f32[2048,512]{1,0:T(8,128)} %copy-done), kind=kLoop, calls=%fused_computation.9 | loop fusion | flops 20969472 | bytes 16793600 | tf_op jit(solution)/shard_map/reduce_max | solution.py:170
  92.4 3.7 %exponential_reduce_fusion = f32[2048]{0:T(1024)S(1)} fusion(f32[2048]{0:T(1024)S(1)} %add_reduce_fusion, f32[2048]{0:T(1024)S(1)} %add_multiply_fusion.3, f32[2048,512]{1,0:T(8,128)S(1)} %copy-done.11, f32[2048,512]{1,0:T(8,128)S(1)} %copy-done.5, f32[2048,512]{1,0:T(8,128)S(1)} %copy-done.8, f32[2048,512]{1,0:T(8,128)S(1)} %copy-done.2), kind=kLoop, calls=%fused_computation.5 | loop fusion | flops 25163776 | bytes 16801792 | tf_op jit(solution)/shard_map/reduce_sum | solution.py:171
  97.8 3.6 %collective-permute-start.13 = (f32[2048]{0:T(1024)S(1)}, f32[2048]{0:T(1024)S(1)}, u32[]{:S(2)}, u32[]{:S(2)}) collective-permute-start(f32[2048]{0:T(1024)S(1)} %bitcast.89), channel_id=1, source_target_pairs={{0,8},{4,12},{8,0},{12,4},{1,9},{5,13},{9,1},{13,5},{2,10},{6,14},... | collective-permute-start | bytes 24584 | tf_op jit(solution)/shard_map/ppermute | solution.py:98
  103.0 2.0 %collective-permute-done.14 = f32[2048]{0:T(1024)S(1)} collective-permute-done((f32[2048]{0:T(1024)S(1)}, f32[2048]{0:T(1024)S(1)}, u32[]{:S(2)}, u32[]{:S(2)}) %collective-permute-start.14) | collective-permute-done | bytes 8224 | tf_op jit(solution)/shard_map/ppermute | solution.py:98
  107.1 21.2 %shard_map.49 = (f32[2048,1]{1,0:T(8,128)}, f32[2048,1]{1,0:T(8,128)}, f32[2048,128]{1,0:T(8,128)}) custom-call(f32[1,2048]{1,0:T(1,128)} %bitcast.87, f32[2048,2048]{1,0:T(8,128)} %get-tuple-element.12.c_ref, f32[2048,128]{1,0:T(8,128)} %pad_maximum_fusion.1.y_ref), custom_call_target="tpu_custom_call" | custom-call | tf_op jit(solution)/shard_map/pallas_call | solution.py:62
  140.4 7.1 %collective-permute-done.20 = f32[512,128]{1,0:T(8,128)S(1)} collective-permute-done((f32[512,128]{1,0:T(8,128)S(1)}, f32[512,128]{1,0:T(8,128)S(1)}, u32[]{:S(2)}, u32[]{:S(2)}) %collective-permute-start.20) | collective-permute-done | bytes 262176 | tf_op jit(solution)/shard_map/ppermute | solution.py:133
  (127 shorter events, 34.3 us)
Async XLA Ops:
  0.6 22.8 %collective-permute-start.1 = (f32[512,128]{1,0:T(8,128)}, f32[512,128]{1,0:T(8,128)S(1)}, u32[]{:S(2)}, u32[]{:S(2)}) collective-permute-start(f32[512,128]{1,0:T(8,128)} %param.5), channel_id=1, source_target_pairs={{0,8},{4,12},{8,0},{12,4},{1,9},{5,13},{9,1},{13,5},{2,10},{6,14},... | collective-permute-start | bytes 786440 | tf_op jit(solution)/shard_map/ppermute | solution.py:152
  4.8 23.0 %collective-permute-start = (f32[512,128]{1,0:T(8,128)}, f32[512,128]{1,0:T(8,128)S(1)}, u32[]{:S(2)}, u32[]{:S(2)}) collective-permute-start(f32[512,128]{1,0:T(8,128)} %param.5), channel_id=1, source_target_pairs={{0,4},{4,8},{8,12},{12,0},{1,5},{5,9},{9,13},{13,1},{2,6},{6,10},{... | collective-permute-start | bytes 786440 | tf_op jit(solution)/shard_map/ppermute | solution.py:152
  6.3 25.9 %collective-permute-start.2 = (f32[512,128]{1,0:T(8,128)}, f32[512,128]{1,0:T(8,128)S(1)}, u32[]{:S(2)}, u32[]{:S(2)}) collective-permute-start(f32[512,128]{1,0:T(8,128)} %param.5), channel_id=1, source_target_pairs={{0,12},{4,0},{8,4},{12,8},{1,13},{5,1},{9,5},{13,9},{2,14},{6,2},{... | collective-permute-start | bytes 786440 | tf_op jit(solution)/shard_map/ppermute | solution.py:152
  16.9 33.7 %copy-start = (f32[2048,512]{1,0:T(8,128)}, f32[2048,512]{1,0:T(8,128)S(1)}, u32[]{:S(2)}) copy-start(f32[2048,512]{1,0:T(8,128)S(1)} %get-tuple-element.34) | copy-start | bytes 12582916
  27.7 22.8 %copy-start.3 = (f32[2048,512]{1,0:T(8,128)}, f32[2048,512]{1,0:T(8,128)S(1)}, u32[]{:S(2)}) copy-start(f32[2048,512]{1,0:T(8,128)S(1)} %get-tuple-element.32) | copy-start | bytes 12582916
  43.8 3.3 %collective-permute-start.3 = (f32[2048]{0:T(1024)S(1)}, f32[2048]{0:T(1024)S(1)}, u32[]{:S(2)}, u32[]{:S(2)}) collective-permute-start(f32[2048]{0:T(1024)S(1)} %log_add_fusion.4), channel_id=1, source_target_pairs={{0,1},{1,2},{2,3},{3,0},{4,5},{5,6},{6,7},{7,4},{8,9},{9,10},{10,1... | collective-permute-start | bytes 24584 | tf_op jit(solution)/shard_map/ppermute | solution.py:98
  43.8 3.7 %collective-permute-start.4 = (f32[2048]{0:T(1024)S(1)}, f32[2048]{0:T(1024)S(1)}, u32[]{:S(2)}, u32[]{:S(2)}) collective-permute-start(f32[2048]{0:T(1024)S(1)} %log_add_fusion.4), channel_id=1, source_target_pairs={{0,2},{1,3},{2,0},{3,1},{4,6},{5,7},{6,4},{7,5},{8,10},{9,11},{10,... | collective-permute-start | bytes 24584 | tf_op jit(solution)/shard_map/ppermute | solution.py:98
  45.7 2.8 %collective-permute-start.5 = (f32[2048]{0:T(1024)S(1)}, f32[2048]{0:T(1024)S(1)}, u32[]{:S(2)}, u32[]{:S(2)}) collective-permute-start(f32[2048]{0:T(1024)S(1)} %log_add_fusion.4), channel_id=1, source_target_pairs={{0,3},{1,0},{2,1},{3,2},{4,7},{5,4},{6,5},{7,6},{8,11},{9,8},{10,9... | collective-permute-start | bytes 24584 | tf_op jit(solution)/shard_map/ppermute | solution.py:98
  54.9 5.7 %collective-permute-start.6 = (f32[2048]{0:T(1024)S(1)}, f32[2048]{0:T(1024)S(1)}, u32[]{:S(2)}, u32[]{:S(2)}) collective-permute-start(f32[2048]{0:T(1024)S(1)} %bitcast.92), channel_id=1, source_target_pairs={{0,4},{4,8},{8,12},{12,0},{1,5},{5,9},{9,13},{13,1},{2,6},{6,10},{... | collective-permute-start | bytes 24584 | tf_op jit(solution)/shard_map/ppermute | solution.py:98
  55.8 4.8 %collective-permute-start.7 = (f32[2048]{0:T(1024)S(1)}, f32[2048]{0:T(1024)S(1)}, u32[]{:S(2)}, u32[]{:S(2)}) collective-permute-start(f32[2048]{0:T(1024)S(1)} %bitcast.93), channel_id=1, source_target_pairs={{0,8},{4,12},{8,0},{12,4},{1,9},{5,13},{9,1},{13,5},{2,10},{6,14},... | collective-permute-start | bytes 24584 | tf_op jit(solution)/shard_map/ppermute | solution.py:98
  57.7 4.2 %collective-permute-start.8 = (f32[2048]{0:T(1024)S(1)}, f32[2048]{0:T(1024)S(1)}, u32[]{:S(2)}, u32[]{:S(2)}) collective-permute-start(f32[2048]{0:T(1024)S(1)} %bitcast.94), channel_id=1, source_target_pairs={{0,12},{4,0},{8,4},{12,8},{1,13},{5,1},{9,5},{13,9},{2,14},{6,2},{... | collective-permute-start | bytes 24584 | tf_op jit(solution)/shard_map/ppermute | solution.py:98
  77.5 3.7 %collective-permute-start.10 = (f32[2048]{0:T(1024)S(1)}, f32[2048]{0:T(1024)S(1)}, u32[]{:S(2)}, u32[]{:S(2)}) collective-permute-start(f32[2048]{0:T(1024)S(1)} %log_add_fusion.2), channel_id=1, source_target_pairs={{0,2},{1,3},{2,0},{3,1},{4,6},{5,7},{6,4},{7,5},{8,10},{9,11},{10,... | collective-permute-start | bytes 24584 | tf_op jit(solution)/shard_map/ppermute | solution.py:98
  78.5 2.8 %collective-permute-start.11 = (f32[2048]{0:T(1024)S(1)}, f32[2048]{0:T(1024)S(1)}, u32[]{:S(2)}, u32[]{:S(2)}) collective-permute-start(f32[2048]{0:T(1024)S(1)} %log_add_fusion.2), channel_id=1, source_target_pairs={{0,3},{1,0},{2,1},{3,2},{4,7},{5,4},{6,5},{7,6},{8,11},{9,8},{10,9... | collective-permute-start | bytes 24584 | tf_op jit(solution)/shard_map/ppermute | solution.py:98
  78.5 3.1 %collective-permute-start.9 = (f32[2048]{0:T(1024)S(1)}, f32[2048]{0:T(1024)S(1)}, u32[]{:S(2)}, u32[]{:S(2)}) collective-permute-start(f32[2048]{0:T(1024)S(1)} %log_add_fusion.2), channel_id=1, source_target_pairs={{0,1},{1,2},{2,3},{3,0},{4,5},{5,6},{6,7},{7,4},{8,9},{9,10},{10,1... | collective-permute-start | bytes 24584 | tf_op jit(solution)/shard_map/ppermute | solution.py:98
  96.7 5.7 %collective-permute-start.12 = (f32[2048]{0:T(1024)S(1)}, f32[2048]{0:T(1024)S(1)}, u32[]{:S(2)}, u32[]{:S(2)}) collective-permute-start(f32[2048]{0:T(1024)S(1)} %bitcast.88), channel_id=1, source_target_pairs={{0,4},{4,8},{8,12},{12,0},{1,5},{5,9},{9,13},{13,1},{2,6},{6,10},{... | collective-permute-start | bytes 24584 | tf_op jit(solution)/shard_map/ppermute | solution.py:98
  97.8 5.2 %collective-permute-start.13 = (f32[2048]{0:T(1024)S(1)}, f32[2048]{0:T(1024)S(1)}, u32[]{:S(2)}, u32[]{:S(2)}) collective-permute-start(f32[2048]{0:T(1024)S(1)} %bitcast.89), channel_id=1, source_target_pairs={{0,8},{4,12},{8,0},{12,4},{1,9},{5,13},{9,1},{13,5},{2,10},{6,14},... | collective-permute-start | bytes 24584 | tf_op jit(solution)/shard_map/ppermute | solution.py:98
  101.4 3.7 %collective-permute-start.14 = (f32[2048]{0:T(1024)S(1)}, f32[2048]{0:T(1024)S(1)}, u32[]{:S(2)}, u32[]{:S(2)}) collective-permute-start(f32[2048]{0:T(1024)S(1)} %bitcast.90), channel_id=1, source_target_pairs={{0,12},{4,0},{8,4},{12,8},{1,13},{5,1},{9,5},{13,9},{2,14},{6,2},{... | collective-permute-start | bytes 24584 | tf_op jit(solution)/shard_map/ppermute | solution.py:98
  129.8 7.0 %collective-permute-start.17 = (f32[2048]{0:T(1024)S(1)}, f32[2048]{0:T(1024)S(1)}, u32[]{:S(2)}, u32[]{:S(2)}) collective-permute-start(f32[2048]{0:T(1024)S(1)} %reduce.25), channel_id=1, source_target_pairs={{0,1},{1,2},{2,3},{3,0},{4,5},{5,6},{6,7},{7,4},{8,9},{9,10},{10,1... | collective-permute-start | bytes 24584 | tf_op jit(solution)/shard_map/ppermute | solution.py:98
  129.9 6.9 %collective-permute-start.18 = (f32[2048]{0:T(1024)S(1)}, f32[2048]{0:T(1024)S(1)}, u32[]{:S(2)}, u32[]{:S(2)}) collective-permute-start(f32[2048]{0:T(1024)S(1)} %reduce.25), channel_id=1, source_target_pairs={{0,2},{1,3},{2,0},{3,1},{4,6},{5,7},{6,4},{7,5},{8,10},{9,11},{10,... | collective-permute-start | bytes 24584 | tf_op jit(solution)/shard_map/ppermute | solution.py:98
  131.1 5.7 %collective-permute-start.19 = (f32[2048]{0:T(1024)S(1)}, f32[2048]{0:T(1024)S(1)}, u32[]{:S(2)}, u32[]{:S(2)}) collective-permute-start(f32[2048]{0:T(1024)S(1)} %reduce.25), channel_id=1, source_target_pairs={{0,3},{1,0},{2,1},{3,2},{4,7},{5,4},{6,5},{7,6},{8,11},{9,8},{10,9... | collective-permute-start | bytes 24584 | tf_op jit(solution)/shard_map/ppermute | solution.py:98
  134.1 1.7 %collective-permute-start.15 = (f32[2,512]{1,0:T(2,128)S(1)}, f32[2,512]{1,0:T(2,128)S(1)}, u32[]{:S(2)}, u32[]{:S(2)}) collective-permute-start(f32[2,512]{1,0:T(2,128)S(1)} %bitcast.108), channel_id=1, source_target_pairs={{0,1},{1,0},{2,3},{3,2},{4,5},{5,4},{6,7},{7,6},{8,9},{9,8},{10,11... | collective-permute-start | bytes 12296 | tf_op jit(solution)/shard_map/ppermute | solution.py:124
  135.3 2.1 %collective-permute-start.16 = (f32[2,512,128]{2,1,0:T(8,128)S(1)}, f32[2,512,128]{2,1,0:T(8,128)S(1)}, u32[]{:S(2)}, u32[]{:S(2)}) collective-permute-start(f32[2,512,128]{2,1,0:T(8,128)S(1)} %dynamic-slice_bitcast_fusion), channel_id=1, source_target_pairs={{0,1},{1,0},{2,3},{3,2},{4,5},{5,4},{6,7},{7,6},{8,9},{9,8},{10,11... | collective-permute-start | bytes 1572872 | tf_op jit(solution)/shard_map/ppermute | solution.py:123
  135.9 4.4 %collective-permute-start.21 = (f32[512]{0:T(512)S(1)}, f32[512]{0:T(512)S(1)}, u32[]{:S(2)}, u32[]{:S(2)}) collective-permute-start(f32[512]{0:T(512)S(1)} %bitcast.109), channel_id=1, source_target_pairs={{0,2},{1,3},{2,0},{3,1},{4,6},{5,7},{6,4},{7,5},{8,10},{9,11},{10,... | collective-permute-start | bytes 6152 | tf_op jit(solution)/shard_map/ppermute | solution.py:134
  138.8 8.7 %collective-permute-start.20 = (f32[512,128]{1,0:T(8,128)S(1)}, f32[512,128]{1,0:T(8,128)S(1)}, u32[]{:S(2)}, u32[]{:S(2)}) collective-permute-start(f32[512,128]{1,0:T(8,128)S(1)} %dynamic-slice_bitcast_fusion.1), channel_id=1, source_target_pairs={{0,2},{1,3},{2,0},{3,1},{4,6},{5,7},{6,4},{7,5},{8,10},{9,11},{10,... | collective-permute-start | bytes 786440 | tf_op jit(solution)/shard_map/ppermute | solution.py:133
  (12 other events, 128.2 us)
